TPU v7x, 512 devices: a whole 4x8x8 slice. The times are simulated.
512 devices in a mesh: rx: 8 (over y), tm: 16 (over z, core), bin: 4 (over x).
Axes of the slice: x: 4, y: 8, z: 8, core: 2. Of those that a mesh axis runs over, the one named last changes fastest.
Arguments:
- samples: bfloat16 [4, 4096, 4096], P('bin', 'tm', 'rx'), may hold values from -45 to 45, as said below
- test_matrix: bfloat16 [4, 4096, 512], P('bin', 'tm'), may hold values from -0.09375 to 0.09375
- forgetting: float32 [4, 16, 512], P('bin', 'tm'), may hold values from 0 to 1, as said below
- prior_sketch: bfloat16 [4, 4096, 512], P('bin', 'rx'), may hold values from -6 to 6
Outputs:
- basis: bfloat16 [4, 16, 4096, 512], P('bin', 'tm', 'rx')
- coefficients: float32 [4, 4096, 512], P('bin', 'tm')
Inputs may be any that keep to these rules, and one draw needn't show every extreme that they name: `samples`: real-valued data. `forgetting`: positive factors.
All inputs are finite; a program needn't handle non-finite values.
Results may differ from a plain program's by a relative error of at most 0.015.
Values may be sent and summed in bfloat16 or wider, within the bound.
No kernel may reach another device: no remote copies, remote signals or barrier semaphores. Data moves between devices by JAX's collectives and lax.ppermute only.
A program may use at most 64 MiB of HBM per device.

v0:
```python
import math

import jax
import jax.numpy as jnp
from jax import lax
from jax.sharding import PartitionSpec as P


def prefix_2(part, axis, combine, identity):
    place = lax.axis_index(axis)
    gathered = jax.tree.map(lambda a: lax.all_gather(a, axis), part)
    state = jax.tree.map(lambda a, e: jnp.zeros_like(a) + jnp.asarray(e, a.dtype), part, identity)

    def one(hop, state):
        return combine(
            state, jax.tree.map(lambda a: lax.dynamic_index_in_dim(a, hop, 0, False), gathered)
        )

    return lax.fori_loop(0, place, one, state)


def with_halo(block, sides, width):
    for axis, dim in sides:
        count = lax.axis_size(axis)
        forward = [(i, i + 1) for i in range(count - 1)]
        backward = [(target, source) for source, target in forward]
        low = lax.ppermute(
            lax.slice_in_dim(block, block.shape[dim] - width, None, axis=dim), axis, forward
        )
        high = lax.ppermute(lax.slice_in_dim(block, 0, width, axis=dim), axis, backward)
        block = jnp.concatenate([low, block, high], axis=dim)
    return block


def combine(earlier, later):
    return (earlier[0] * later[0], later[0][None, :] * earlier[1] + later[1])


def sketch_of(block_data, block_test):
    return lax.dot_general(
        block_data, block_test, (((0,), (0,)), ((), ())), preferred_element_type=jnp.float32
    )


def body(samples, test_matrix, forgetting, prior_sketch):
    block_data = samples[0]
    block_test = test_matrix[0]
    own_decay = forgetting[0, 0]
    prior_rows = prior_sketch[0].astype(jnp.float32)
    width = block_test.shape[1]
    rows = block_data.shape[1]
    steps = lax.axis_size("tm")
    place = lax.axis_index("tm")
    gathered = lax.all_gather(
        jnp.concatenate([block_data, block_test], axis=1), "tm", axis=0, tiled=True
    )
    all_data = gathered[:, :rows]
    all_test = gathered[:, rows:]
    decays = lax.all_gather(own_decay, "tm", axis=0)
    owner = lax.broadcasted_iota(jnp.int32, (steps, steps, 1), 0)
    later = lax.broadcasted_iota(jnp.int32, (steps, steps, 1), 1)
    inside = (later > owner) & (later <= place)
    weight = jnp.prod(jnp.where(inside, decays[None], 1.0), axis=1)
    weight = jnp.where(owner[:, 0] <= place, weight, 0.0)
    prior_weight = jnp.prod(jnp.where(later[0] <= place, decays, 1.0), axis=0)
    cols = block_test.shape[0]
    scaled = (all_test.reshape(steps, cols, width).astype(jnp.float32) * weight[:, None, :]).reshape(
        steps * cols, width
    )
    high = scaled.astype(jnp.bfloat16)
    low = (scaled - high.astype(jnp.float32)).astype(jnp.bfloat16)
    both = lax.dot_general(
        all_data,
        jnp.concatenate([high, low], axis=1),
        (((0,), (0,)), ((), ())),
        preferred_element_type=jnp.float32,
    )
    prefix = both[:, :width] + both[:, width:] + prior_weight[None, :] * prior_rows
    padded = with_halo(prefix[None], (("bin", 0),), 1)
    mixed = padded[1] + 0.25 * (padded[0] + padded[2])
    local_gram = lax.dot_general(
        mixed,
        mixed,
        (((0,), (0,)), ((), ())),
        precision=lax.Precision.HIGHEST,
        preferred_element_type=jnp.float32,
    )
    local_proj = jnp.dot(
        block_data.astype(jnp.float32),
        mixed,
        precision=lax.Precision.HIGHEST,
        preferred_element_type=jnp.float32,
    )
    summed = lax.psum(jnp.concatenate([local_gram, local_proj], axis=0), "rx")
    gram = summed[:width]
    factor = jnp.linalg.cholesky(gram)
    solved = jax.scipy.linalg.solve_triangular(
        factor, jnp.concatenate([mixed, summed[width:]], axis=0).T, lower=True
    ).T
    ortho = solved[:rows]
    coords = solved[rows:]
    receivers = rows * lax.axis_size("rx")
    basis = (math.sqrt(receivers) * ortho).astype(jnp.bfloat16)
    return (basis[None, None], coords[None])


def solution(mesh):
    return jax.shard_map(
        body,
        mesh=mesh,
        in_specs=(
            P("bin", "tm", "rx"),
            P("bin", "tm", None),
            P("bin", "tm", None),
            P("bin", "rx", None),
        ),
        out_specs=(P("bin", "tm", "rx", None), P("bin", "tm", None)),
        check_vma=False,
    )
```

profile of v0, /device:TPU:6, one launch (start us, length us, event | category | flops | bytes accessed | tf_op | source)
XLA Modules:
  0.0 365.5 jit_solution(161297435252849803)
XLA Ops:
  7.2 1.9 pad_maximum_fusion.1
  9.2 23.5 %all-gather = f32[16,1,512]{2,1,0:T(1,128)S(1)} all-gather(f32[1,1,512]{2,1,0:T(1,128)} %param.6), channel_id=2, replica_groups=mesh['rx'=8,'tm'=16,'bin'=4] {'tm'}, dimensions={0}, use_global_device_ids=true | all-gather | bytes 34816 | tf_op jit(solution)/shard_map/all_gather | solution.py:59
  33.0 41.5 %all-gather.3.cloned.1.call-done = bf16[4096,1024]{1,0:T(8,128)(2,1)} async-done(((bf16[256,1024]{1,0:T(8,128)(2,1)}), bf16[4096,1024]{1,0:T(8,128)(2,1)}) %all-gather.3.cloned.1.call-update) | async-done | bytes 8388624 | tf_op jit(solution)/shard_map/all_gather | solution.py:54
  74.6 3.0 fusion.4
  79.2 4.5 %fusion = f32[512,1024]{1,0:T(8,128)S(1)} fusion(bf16[4096,512]{1,0:T(8,128)(2,1)S(1)} %get-tuple-element.27, bf16[4096,512]{1,0:T(8,128)(2,1)S(1)} %get-tuple-element.26, bf16[4096,1024]{1,0:T(8,128)(2,1)S(1)} %copy-done.1), kind=kOutput, calls=%fused_computation.2 | convolution fusion | flops 4311744512 | bytes 14680064 | tf_op jit(solution)/shard_map/dot_general | solution.py:72
  85.5 5.1 %collective-permute-start.1 = (f32[1,512,512]{2,1,0:T(8,128)S(1)}, f32[1,512,512]{2,1,0:T(8,128)S(1)}, u32[]{:S(2)}, u32[]{:S(2)}) collective-permute-start(f32[1,512,512]{2,1,0:T(8,128)S(1)} %fusion.42), channel_id=1, source_target_pairs={{1,0},{2,1},{3,2},{5,4},{6,5},{7,6},{9,8},{10,9},{11,10},{13,12},{... | collective-permute-start | bytes 3145736 | tf_op jit(solution)/shard_map/ppermute | solution.py:30
  90.6 20.8 %collective-permute-done = f32[1,512,512]{2,1,0:T(8,128)S(1)} collective-permute-done((f32[1,512,512]{2,1,0:T(8,128)S(1)}, f32[1,512,512]{2,1,0:T(8,128)S(1)}, u32[]{:S(2)}, u32[]{:S(2)}) %collective-permute-start) | collective-permute-done | bytes 1048608 | tf_op jit(solution)/shard_map/ppermute | solution.py:27
  114.1 1.9 fusion.44
  117.3 83.6 %all-reduce.3.cloned.1.call-done = f32[768,512]{0,1:T(8,128)} async-done(((f32[768,512]{0,1:T(8,128)}), f32[768,512]{0,1:T(8,128)}) %all-reduce.3.cloned.1.call-update) | async-done | bytes 1572880 | tf_op jit(solution)/shard_map/psum | solution.py:94
  207.6 11.7 %cholesky.104 = f32[128,128]{1,0:T(8,128)S(1)} custom-call(f32[128,128]{1,0:T(8,128)S(1)} %cholesky.266), custom_call_target="Cholesky" | custom-call | tf_op jit(solution)/shard_map/jit(cholesky)/cholesky | solution.py:96
  219.4 9.8 %custom-call.31 = f32[1,128,128]{1,2,0:T(8,128)S(1)} custom-call(f32[1,128,128]{2,1,0:T(8,128)S(1)} %get-tuple-element.37), custom_call_target="InvertDiagBlocksLowerTriangular" | custom-call | tf_op jit(solution)/shard_map/jit(cholesky)/cholesky | solution.py:96
  231.8 11.9 %cholesky.217 = f32[128,128]{1,0:T(8,128)S(1)} custom-call(f32[128,128]{1,0:T(8,128)S(1)} %cholesky.270), custom_call_target="Cholesky" | custom-call | tf_op jit(solution)/shard_map/jit(cholesky)/cholesky | solution.py:96
  243.7 9.8 %custom-call.32 = f32[1,128,128]{1,2,0:T(8,128)S(1)} custom-call(f32[1,128,128]{2,1,0:T(8,128)S(1)} %get-tuple-element.34), custom_call_target="InvertDiagBlocksLowerTriangular" | custom-call | tf_op jit(solution)/shard_map/jit(cholesky)/cholesky | solution.py:96
  255.1 11.7 %cholesky.238 = f32[128,128]{1,0:T(8,128)S(1)} custom-call(f32[128,128]{1,0:T(8,128)S(1)} %cholesky.275), custom_call_target="Cholesky" | custom-call | tf_op jit(solution)/shard_map/jit(cholesky)/cholesky | solution.py:96
  266.8 9.8 %custom-call.33 = f32[1,128,128]{1,2,0:T(8,128)S(1)} custom-call(f32[1,128,128]{2,1,0:T(8,128)S(1)} %get-tuple-element.31), custom_call_target="InvertDiagBlocksLowerTriangular" | custom-call | tf_op jit(solution)/shard_map/jit(cholesky)/cholesky | solution.py:96
  278.1 11.9 %cholesky.255 = f32[128,128]{1,0:T(8,128)S(1)} custom-call(f32[128,128]{1,0:T(8,128)S(1)} %convolution_subtract_fusion.5), custom_call_target="Cholesky" | custom-call | tf_op jit(solution)/shard_map/jit(cholesky)/cholesky | solution.py:96
  295.7 12.0 %while.1 = (s32[]{:T(128)}, f32[512,512]{1,0:T(8,128)}, s32[4,2]{0,1:T(2,128)S(1)}, f32[4,128,128]{2,1,0:T(8,128)S(1)}, s32[]{:T(128)}) while((s32[]{:T(128)}, f32[512,512]{1,0:T(8,128)}, s32[4,2]{0,1:T(2,128)S(1)}, f32[4,128,128]{2,1,0:T(8,128)S(1)}, s32[]{:T(128)}) %tuple.35), condition=%wide.while_cond, body=%wide.while_body.sunk | while | flops 2 | bytes 131189 | solution.py:97
  296.4 2.3 bitcast_dynamic-update-slice_fusion.2
  299.4 2.3 bitcast_dynamic-update-slice_fusion.2
  302.4 2.3 bitcast_dynamic-update-slice_fusion.2
  305.4 2.3 bitcast_dynamic-update-slice_fusion.2
  307.7 39.3 %custom-call.34 = f32[4,128,128]{1,2,0:T(8,128)S(1)} custom-call(f32[4,128,128]{2,1,0:T(8,128)S(1)} %get-tuple-element.9), custom_call_target="InvertDiagBlocksLowerTriangular" | custom-call | tf_op jit(solution)/shard_map/jit(_solve_triangular)/triangular_solve | solution.py:97
  349.8 2.3 convolution_subtract_fusion.2
  352.6 3.0 convolution_subtract_fusion
  (71 shorter events, 32.0 us)
Async XLA Ops:
  7.2 67.4 %all-gather.3.cloned.1.call-start = ((), (), s32[]{:S(2)}) async-start(), calls=%async_computation | async-start | bytes 8912896 | tf_op jit(solution)/shard_map/all_gather | solution.py:54
  9.1 191.7 %all-reduce.3.cloned.1.call-start = ((), (), s32[]{:S(2)}) async-start(), calls=%async_computation.1 | async-start | bytes 3145728 | tf_op jit(solution)/shard_map/psum | solution.py:94
  74.6 4.7 %copy-start.1 = (bf16[4096,1024]{1,0:T(8,128)(2,1)S(1)}, bf16[4096,1024]{1,0:T(8,128)(2,1)}, u32[]{:S(2)}) copy-start(bf16[4096,1024]{1,0:T(8,128)(2,1)} %all-gather.3.cloned.1.call-done) | copy-start | bytes 25165828
  79.2 4.5 %copy-start.2 = (bf16[1,512,512]{2,1,0:T(8,128)(2,1)S(1)}, bf16[1,512,512]{2,1,0:T(8,128)(2,1)}, u32[]{:S(2)}) copy-start(bf16[1,512,512]{2,1,0:T(8,128)(2,1)} %param.7) | copy-start | bytes 1572868
  84.0 29.1 %copy-start.3 = (bf16[1,256,512]{2,1,0:T(8,128)(2,1)S(1)}, bf16[1,256,512]{2,1,0:T(8,128)(2,1)}, u32[]{:S(2)}) copy-start(bf16[1,256,512]{2,1,0:T(8,128)(2,1)} %param.4) | copy-start | bytes 786436
  84.0 27.3 %collective-permute-start = (f32[1,512,512]{2,1,0:T(8,128)S(1)}, f32[1,512,512]{2,1,0:T(8,128)S(1)}, u32[]{:S(2)}, u32[]{:S(2)}) collective-permute-start(f32[1,512,512]{2,1,0:T(8,128)S(1)} %fusion.42), channel_id=1, source_target_pairs={{0,1},{1,2},{2,3},{4,5},{5,6},{6,7},{8,9},{9,10},{10,11},{12,13},{... | collective-permute-start | bytes 3145736 | tf_op jit(solution)/shard_map/ppermute | solution.py:27
  85.5 27.1 %collective-permute-start.1 = (f32[1,512,512]{2,1,0:T(8,128)S(1)}, f32[1,512,512]{2,1,0:T(8,128)S(1)}, u32[]{:S(2)}, u32[]{:S(2)}) collective-permute-start(f32[1,512,512]{2,1,0:T(8,128)S(1)} %fusion.42), channel_id=1, source_target_pairs={{1,0},{2,1},{3,2},{5,4},{6,5},{7,6},{9,8},{10,9},{11,10},{13,12},{... | collective-permute-start | bytes 3145736 | tf_op jit(solution)/shard_map/ppermute | solution.py:30
  202.3 1.2 slice-start
  206.5 1.0 copy-start
Sparse Core Ops, SparseCore 0:
  10.7 63.8 all-gather.2
  117.4 83.4 all-reduce.2
where the time goes:
time: 370 us; the launch traced here: 366 us
  waiting for transfers between devices  147 us (40%)
  other arithmetic  129 us (35%)
  blocking collectives  23.5 us (6%)
  matrix products  22 us (6%)
  local copies, waits for them, and re-layouts  20.6 us (6%)
  between operations  17.1 us (5%)
  starting transfers between devices  6.58 us (2%)
    psum x1, waiting for transfers between devices, body(): summed = lax.psum(jnp.concatenate([local_gram, local_proj], axis=0), 'rx')  83.6 us
    another operation x14, other arithmetic, body(): factor = jnp.linalg.cholesky(gram)  78.8 us
    all_gather x1, waiting for transfers between devices, body(): lax.all_gather(jnp.concatenate([block_data, block_test], axis=1), 'tm', a...  41.5 us
    another operation x3, other arithmetic, body(): jax.scipy.linalg.solve_triangular(factor, jnp.concatenate([mixed, summed[...  40.4 us
    all_gather x1, blocking collectives, body(): decays = lax.all_gather(own_decay, 'tm', axis=0)  23.5 us
    ppermute x1, waiting for transfers between devices, with_halo(): lax.ppermute(lax.slice_in_dim(block, block.shape[dim] - width, None, axis...  20.8 us
    another operation x12, local copies, waits for them, and re-layouts  12 us
    another operation x7, matrix products, body(): jax.scipy.linalg.solve_triangular(factor, jnp.concatenate([mixed, summed[...  9.11 us
  transfers between devices with their start and end apart: 4, of which 4 were waited for; matrix products, arithmetic and copies ran while one was open for 0% of the time, Pallas kernels for 0%

commit v1 on v0

--- a/solution.py
+++ b/solution.py
@@ -30,6 +30,43 @@
         high = lax.ppermute(lax.slice_in_dim(block, 0, width, axis=dim), axis, backward)
         block = jnp.concatenate([low, block, high], axis=dim)
     return block
+
+
+def blocked_factor(gram, block):
+    size = gram.shape[0]
+    count = size // block
+    hi = lax.Precision.HIGHEST
+    eye = jnp.eye(block, dtype=gram.dtype)
+    columns = []
+    inverses = []
+    for j in range(count):
+        top, end = j * block, (j + 1) * block
+        panel = gram[top:, top:end]
+        if j:
+            done = jnp.concatenate([c[top - c_top:] for c_top, c in columns], axis=1)
+            panel = panel - jnp.dot(done, done[:block].T, precision=hi)
+        diag = lax.linalg.cholesky(panel[:block], symmetrize_input=True)
+        inverse = jnp.tril(lax.linalg.triangular_solve(diag, eye, left_side=True, lower=True))
+        inverses.append(inverse)
+        if j + 1 < count:
+            below = jnp.dot(panel[block:], inverse.T, precision=hi)
+            columns.append((top, jnp.concatenate([diag, below], axis=0)))
+        else:
+            columns.append((top, diag))
+    return columns, inverses
+
+
+def right_solve(values, columns, inverses, block):
+    hi = lax.Precision.HIGHEST
+    parts = []
+    for j, inverse in enumerate(inverses):
+        top = j * block
+        part = values[:, top:top + block]
+        for k in range(j):
+            c_top, col = columns[k]
+            part = part - jnp.dot(parts[k], col[top - c_top:top - c_top + block].T, precision=hi)
+        parts.append(jnp.dot(part, inverse.T, precision=hi))
+    return jnp.concatenate(parts, axis=1)
 
 
 def combine(earlier, later):
@@ -93,10 +130,11 @@
     )
     summed = lax.psum(jnp.concatenate([local_gram, local_proj], axis=0), "rx")
     gram = summed[:width]
-    factor = jnp.linalg.cholesky(gram)
-    solved = jax.scipy.linalg.solve_triangular(
-        factor, jnp.concatenate([mixed, summed[width:]], axis=0).T, lower=True
-    ).T
+    block = 128
+    columns, inverses = blocked_factor(gram, block)
+    solved = right_solve(
+        jnp.concatenate([mixed, summed[width:]], axis=0), columns, inverses, block
+    )
     ortho = solved[:rows]
     coords = solved[rows:]
     receivers = rows * lax.axis_size("rx")

time: 370 us -> 328 us (0.89)
  other arithmetic: 129 us -> 101 us
  local copies, waits for them, and re-layouts: 20.6 us -> 6.72 us
    another operation x17 -> x20, other arithmetic: 119 us -> 91.8 us  [the longest x12 49.9 us: blocked_factor(): diag = lax.linalg.cholesky(panel[:block], symmetrize_input=True)]
    ppermute x1, waiting for transfers between devices: 1.18 us -> 21 us  [with_halo(): lax.ppermute(lax.slice_in_dim(block, 0, width, axis=dim), axis, backward)]
    ppermute x1, waiting for transfers between devices: 20.8 us -> 4.18 us  [with_halo(): lax.ppermute(lax.slice_in_dim(block, block.shape[dim] - width, None, axis...]
    dot_general x0 -> x16, matrix products: none -> 15.8 us  [the longest x6 6.43 us: right_solve(): jnp.dot(parts[k], col[top - c_top:top - c_top + block].T, precision=hi)]
    another operation x13 -> x4, matrix products: 14.6 us -> 1.14 us  [blocked_factor(): lax.linalg.triangular_solve(diag, eye, left_side=True, lower=True)]
    another operation x17 -> x0, local copies, waits for them, and re-layouts: 12.1 us -> none
where the time goes in v1:
time: 328 us; the launch traced here: 324 us
  waiting for transfers between devices  148 us (45%)
  other arithmetic  101 us (31%)
  matrix products  24.3 us (7%)
  blocking collectives  23.5 us (7%)
  between operations  14.8 us (5%)
  local copies, waits for them, and re-layouts  6.72 us (2%)
  starting transfers between devices  4.85 us (1%)
    psum x1, waiting for transfers between devices, body(): summed = lax.psum(jnp.concatenate([local_gram, local_proj], axis=0), 'rx')  81.6 us
    another operation x12, other arithmetic, blocked_factor(): diag = lax.linalg.cholesky(panel[:block], symmetrize_input=True)  49.9 us
    another operation x8, other arithmetic, blocked_factor(): lax.linalg.triangular_solve(diag, eye, left_side=True, lower=True)  41.9 us
    all_gather x1, waiting for transfers between devices, body(): lax.all_gather(jnp.concatenate([block_data, block_test], axis=1), 'tm', a...  41.5 us
    all_gather x1, blocking collectives, body(): decays = lax.all_gather(own_decay, 'tm', axis=0)  23.5 us
    ppermute x1, waiting for transfers between devices, with_halo(): lax.ppermute(lax.slice_in_dim(block, 0, width, axis=dim), axis, backward)  21 us
  transfers between devices with their start and end apart: 4, of which 4 were waited for; matrix products, arithmetic and copies ran while one was open for 0% of the time, Pallas kernels for 0%

profile of v1, /device:TPU:6, one launch (start us, length us, event | category | flops | bytes accessed | tf_op | source)
XLA Modules:
  0.0 323.6 jit_solution(10479919024083043111)
XLA Ops:
  7.2 1.9 pad_maximum_fusion.2
  9.2 23.5 %all-gather = f32[16,1,512]{2,1,0:T(1,128)S(1)} all-gather(f32[1,1,512]{2,1,0:T(1,128)} %param.9), channel_id=2, replica_groups=mesh['rx'=8,'tm'=16,'bin'=4] {'tm'}, dimensions={0}, use_global_device_ids=true | all-gather | bytes 34816 | tf_op jit(solution)/shard_map/all_gather | solution.py:96
  33.0 41.5 %all-gather.3.cloned.1.call-done = bf16[4096,1024]{1,0:T(8,128)(2,1)} async-done(((bf16[256,1024]{1,0:T(8,128)(2,1)}), bf16[4096,1024]{1,0:T(8,128)(2,1)}) %all-gather.3.cloned.1.call-update) | async-done | bytes 8388624 | tf_op jit(solution)/shard_map/all_gather | solution.py:91
  74.6 3.0 fusion.4
  77.6 1.7 copy-done.1
  79.2 4.5 %fusion = f32[512,1024]{1,0:T(8,128)S(1)} fusion(bf16[4096,512]{1,0:T(8,128)(2,1)S(1)} %get-tuple-element.11, bf16[4096,512]{1,0:T(8,128)(2,1)S(1)} %get-tuple-element.10, bf16[4096,1024]{1,0:T(8,128)(2,1)S(1)} %copy-done.1), kind=kOutput, calls=%fused_computation | convolution fusion | flops 4311744512 | bytes 14680064 | tf_op jit(solution)/shard_map/dot_general | solution.py:109
  84.0 3.0 collective-permute-start.1
  87.1 1.8 collective-permute-start
  88.8 21.0 %collective-permute-done.1 = f32[1,512,512]{2,1,0:T(8,128)S(1)} collective-permute-done((f32[1,512,512]{2,1,0:T(8,128)S(1)}, f32[1,512,512]{2,1,0:T(8,128)S(1)}, u32[]{:S(2)}, u32[]{:S(2)}) %collective-permute-start.1) | collective-permute-done | bytes 1048608 | tf_op jit(solution)/shard_map/ppermute | solution.py:30
  109.8 4.2 %collective-permute-done = f32[1,512,512]{2,1,0:T(8,128)S(1)} collective-permute-done((f32[1,512,512]{2,1,0:T(8,128)S(1)}, f32[1,512,512]{2,1,0:T(8,128)S(1)}, u32[]{:S(2)}, u32[]{:S(2)}) %collective-permute-start) | collective-permute-done | bytes 1048608 | tf_op jit(solution)/shard_map/ppermute | solution.py:27
  115.5 1.9 fusion.59
  118.7 81.6 %all-reduce.2.cloned.1.call-done = f32[768,512]{0,1:T(8,128)} async-done(((f32[768,512]{0,1:T(8,128)}), f32[768,512]{0,1:T(8,128)}) %all-reduce.2.cloned.1.call-update) | async-done | bytes 1572880 | tf_op jit(solution)/shard_map/psum | solution.py:131
  202.3 11.7 %custom-call.12 = f32[128,128]{1,0:T(8,128)S(1)} custom-call(f32[128,128]{1,0:T(8,128)S(1)} %copy.45), custom_call_target="Cholesky" | custom-call | tf_op jit(solution)/shard_map/cholesky/custom-call.1 | solution.py:48
  215.3 9.8 %custom-call.13 = f32[1,128,128]{1,2,0:T(8,128)S(1)} custom-call(f32[1,128,128]{2,1,0:T(8,128)S(1)} %fusion.33), custom_call_target="InvertDiagBlocksLowerTriangular" | custom-call | tf_op jit(solution)/shard_map/triangular_solve/custom-call.0 | solution.py:49
  227.4 1.5 convolution_subtract_fusion.2
  229.9 1.5 convolution_subtract_fusion.5
  232.1 11.7 %custom-call.14 = f32[128,128]{1,0:T(8,128)S(1)} custom-call(f32[128,128]{1,0:T(8,128)S(1)} %copy.49), custom_call_target="Cholesky" | custom-call | tf_op jit(solution)/shard_map/cholesky/custom-call.1 | solution.py:48
  245.2 9.8 %custom-call.15 = f32[1,128,128]{1,2,0:T(8,128)S(1)} custom-call(f32[1,128,128]{2,1,0:T(8,128)S(1)} %fusion.34), custom_call_target="InvertDiagBlocksLowerTriangular" | custom-call | tf_op jit(solution)/shard_map/triangular_solve/custom-call.0 | solution.py:49
  260.1 11.9 %custom-call.16 = f32[128,128]{1,0:T(8,128)S(1)} custom-call(f32[128,128]{1,0:T(8,128)S(1)} %fusion.43), custom_call_target="Cholesky" | custom-call | tf_op jit(solution)/shard_map/cholesky/custom-call.1 | solution.py:48
  273.4 9.8 %custom-call.17 = f32[1,128,128]{1,2,0:T(8,128)S(1)} custom-call(f32[1,128,128]{2,1,0:T(8,128)S(1)} %fusion.35), custom_call_target="InvertDiagBlocksLowerTriangular" | custom-call | tf_op jit(solution)/shard_map/triangular_solve/custom-call.0 | solution.py:49
  284.6 1.4 convolution_subtract_fusion.8
  286.3 11.7 %custom-call.18 = f32[128,128]{1,0:T(8,128)S(1)} custom-call(f32[128,128]{1,0:T(8,128)S(1)} %broadcast_multiply_fusion), custom_call_target="Cholesky" | custom-call | tf_op jit(solution)/shard_map/cholesky/custom-call.1 | solution.py:48
  299.4 9.8 %custom-call.19 = f32[1,128,128]{1,2,0:T(8,128)S(1)} custom-call(f32[1,128,128]{2,1,0:T(8,128)S(1)} %fusion.36), custom_call_target="InvertDiagBlocksLowerTriangular" | custom-call | tf_op jit(solution)/shard_map/triangular_solve/custom-call.0 | solution.py:49
  309.5 1.3 fusion.60
  (91 shorter events, 27.3 us)
Async XLA Ops:
  7.2 67.4 %all-gather.3.cloned.1.call-start = ((), (), s32[]{:S(2)}) async-start(), calls=%async_computation | async-start | bytes 8912896 | tf_op jit(solution)/shard_map/all_gather | solution.py:91
  9.1 191.2 %all-reduce.2.cloned.1.call-start = ((), (), s32[]{:S(2)}) async-start(), calls=%async_computation.1 | async-start | bytes 3145728 | tf_op jit(solution)/shard_map/psum | solution.py:131
  74.6 4.7 %copy-start.1 = (bf16[4096,1024]{1,0:T(8,128)(2,1)S(1)}, bf16[4096,1024]{1,0:T(8,128)(2,1)}, u32[]{:S(2)}) copy-start(bf16[4096,1024]{1,0:T(8,128)(2,1)} %all-gather.3.cloned.1.call-done) | copy-start | bytes 25165828
  79.2 4.5 %copy-start.4 = (bf16[1,512,512]{2,1,0:T(8,128)(2,1)S(1)}, bf16[1,512,512]{2,1,0:T(8,128)(2,1)}, u32[]{:S(2)}) copy-start(bf16[1,512,512]{2,1,0:T(8,128)(2,1)} %param.10) | copy-start | bytes 1572868
  84.0 30.5 %copy-start.8 = (bf16[1,256,512]{2,1,0:T(8,128)(2,1)S(1)}, bf16[1,256,512]{2,1,0:T(8,128)(2,1)}, u32[]{:S(2)}) copy-start(bf16[1,256,512]{2,1,0:T(8,128)(2,1)} %param.7) | copy-start | bytes 786436
  84.0 25.8 %collective-permute-start.1 = (f32[1,512,512]{2,1,0:T(8,128)S(1)}, f32[1,512,512]{2,1,0:T(8,128)S(1)}, u32[]{:S(2)}, u32[]{:S(2)}) collective-permute-start(f32[1,512,512]{2,1,0:T(8,128)S(1)} %fusion.58), channel_id=1, source_target_pairs={{1,0},{2,1},{3,2},{5,4},{6,5},{7,6},{9,8},{10,9},{11,10},{13,12},{... | collective-permute-start | bytes 3145736 | tf_op jit(solution)/shard_map/ppermute | solution.py:30
  87.1 26.9 %collective-permute-start = (f32[1,512,512]{2,1,0:T(8,128)S(1)}, f32[1,512,512]{2,1,0:T(8,128)S(1)}, u32[]{:S(2)}, u32[]{:S(2)}) collective-permute-start(f32[1,512,512]{2,1,0:T(8,128)S(1)} %fusion.58), channel_id=1, source_target_pairs={{0,1},{1,2},{2,3},{4,5},{5,6},{6,7},{8,9},{9,10},{10,11},{12,13},{... | collective-permute-start | bytes 3145736 | tf_op jit(solution)/shard_map/ppermute | solution.py:27
  200.3 26.4 %slice-start.1 = ((f32[768,512]{0,1:T(8,128)}), f32[256,512]{0,1:T(8,128)S(1)}, s32[]{:S(2)}) async-start(f32[768,512]{0,1:T(8,128)} %all-reduce.2.cloned.1.call-done), calls=%async_computation.3 | async-start | bytes 1048576 | tf_op jit(solution)/shard_map/slice | solution.py:136
  226.7 4.8 %copy-start = (f32[384,128]{0,1:T(8,128)}, f32[384,128]{0,1:T(8,128)S(1)}, u32[]{:S(2)}) copy-start(f32[384,128]{0,1:T(8,128)S(1)} %fusion.17) | copy-start | bytes 589828
  229.0 2.5 copy-start.2
  231.9 23.2 %copy-start.7 = (f32[384,128]{0,1:T(8,128)}, f32[384,128]{0,1:T(8,128)S(1)}, u32[]{:S(2)}) copy-start(f32[384,128]{0,1:T(8,128)S(1)} %convolution_subtract_fusion.6) | copy-start | bytes 589828
  231.9 52.7 %slice-start = ((f32[384,128]{0,1:T(8,128)}), f32[128,128]{0,1:T(8,128)S(1)}, s32[]{:S(2)}) async-start(f32[384,128]{0,1:T(8,128)} %copy-done), calls=%async_computation.2 | async-start | bytes 131072 | tf_op jit(solution)/shard_map/slice | solution.py:67
  231.9 52.7 %copy-start.3 = (f32[768,512]{0,1:T(8,128)S(1)}, f32[768,512]{0,1:T(8,128)}, u32[]{:S(2)}) copy-start(f32[768,512]{0,1:T(8,128)} %all-reduce.2.cloned.1.call-done) | copy-start | bytes 4718596
  232.0 77.5 %copy-start.6 = (f32[768,128]{1,0:T(8,128)S(1)}, f32[768,128]{1,0:T(8,128)}, u32[]{:S(2)}) copy-start(f32[768,128]{1,0:T(8,128)} %convolution_subtract_fusion.5) | copy-start | bytes 1179652
  255.3 27.9 %copy-start.10 = (f32[128,128]{1,0:T(8,128)}, f32[128,128]{1,0:T(8,128)S(1)}, u32[]{:S(2)}) copy-start(f32[128,128]{1,0:T(8,128)S(1)} %convolution_select_fusion.2) | copy-start | bytes 196612
  255.3 55.6 %copy-start.5 = (f32[768,128]{1,0:T(8,128)S(1)}, f32[768,128]{1,0:T(8,128)}, u32[]{:S(2)}) copy-start(f32[768,128]{1,0:T(8,128)} %convolution_subtract_fusion.2) | copy-start | bytes 1179652
  258.5 0.7 copy-start.9
Sparse Core Ops, SparseCore 0:
  10.7 63.8 all-gather.2
  118.8 81.4 all-reduce.1

commit v2 on v1

--- a/solution.py
+++ b/solution.py
@@ -104,8 +104,9 @@
     scaled = (all_test.reshape(steps, cols, width).astype(jnp.float32) * weight[:, None, :]).reshape(
         steps * cols, width
     )
-    high = scaled.astype(jnp.bfloat16)
-    low = (scaled - high.astype(jnp.float32)).astype(jnp.bfloat16)
+    rounded = lax.reduce_precision(scaled, exponent_bits=8, mantissa_bits=7)
+    high = rounded.astype(jnp.bfloat16)
+    low = (scaled - rounded).astype(jnp.bfloat16)
     both = lax.dot_general(
         all_data,
         jnp.concatenate([high, low], axis=1),
@@ -113,8 +114,13 @@
         preferred_element_type=jnp.float32,
     )
     prefix = both[:, :width] + both[:, width:] + prior_weight[None, :] * prior_rows
-    padded = with_halo(prefix[None], (("bin", 0),), 1)
-    mixed = padded[1] + 0.25 * (padded[0] + padded[2])
+    bins = lax.axis_size("bin")
+    upward = [(i, i + 1) for i in range(bins - 1)]
+    downward = [(b, a) for a, b in upward]
+    sent = prefix.astype(jnp.bfloat16)
+    below = lax.ppermute(sent, "bin", upward).astype(jnp.float32)
+    above = lax.ppermute(sent, "bin", downward).astype(jnp.float32)
+    mixed = prefix + 0.25 * (below + above)
     local_gram = lax.dot_general(
         mixed,
         mixed,

time: 328 us -> 317 us (0.966)
  waiting for transfers between devices: 148 us -> 137 us
    ppermute x2, waiting for transfers between devices: 25.2 us -> 13.9 us  [the longest x1 9.77 us: body(): above = lax.ppermute(sent, 'bin', downward).astype(jnp.float32)]
where the time goes in v2:
time: 317 us; the launch traced here: 312 us
  waiting for transfers between devices  137 us (43%)
  other arithmetic  101 us (32%)
  matrix products  24.4 us (8%)
  blocking collectives  23.5 us (7%)
  between operations  14.8 us (5%)
  local copies, waits for them, and re-layouts  6.48 us (2%)
  starting transfers between devices  4.82 us (2%)
    psum x1, waiting for transfers between devices, body(): summed = lax.psum(jnp.concatenate([local_gram, local_proj], axis=0), 'rx')  81.6 us
    another operation x12, other arithmetic, blocked_factor(): diag = lax.linalg.cholesky(panel[:block], symmetrize_input=True)  49.9 us
    another operation x8, other arithmetic, blocked_factor(): lax.linalg.triangular_solve(diag, eye, left_side=True, lower=True)  41.9 us
    all_gather x1, waiting for transfers between devices, body(): lax.all_gather(jnp.concatenate([block_data, block_test], axis=1), 'tm', a...  41.5 us
    all_gather x1, blocking collectives, body(): decays = lax.all_gather(own_decay, 'tm', axis=0)  23.5 us
    ppermute x1, waiting for transfers between devices, body(): above = lax.ppermute(sent, 'bin', downward).astype(jnp.float32)  9.77 us
    dot_general x6, matrix products, right_solve(): jnp.dot(parts[k], col[top - c_top:top - c_top + block].T, precision=hi)  6.43 us
  transfers between devices with their start and end apart: 4, of which 4 were waited for; matrix products, arithmetic and copies ran while one was open for 0% of the time, Pallas kernels for 0%

profile of v2, /device:TPU:6, one launch (start us, length us, event | category | flops | bytes accessed | tf_op | source)
XLA Modules:
  0.0 312.3 jit_solution(10678677387707663500)
XLA Ops:
  7.2 1.9 pad_maximum_fusion.2
  9.2 23.5 %all-gather = f32[16,1,512]{2,1,0:T(1,128)S(1)} all-gather(f32[1,1,512]{2,1,0:T(1,128)} %param.9), channel_id=2, replica_groups=mesh['rx'=8,'tm'=16,'bin'=4] {'tm'}, dimensions={0}, use_global_device_ids=true | all-gather | bytes 34816 | tf_op jit(solution)/shard_map/all_gather | solution.py:96
  33.0 41.5 %all-gather.3.cloned.1.call-done = bf16[4096,1024]{1,0:T(8,128)(2,1)} async-done(((bf16[256,1024]{1,0:T(8,128)(2,1)}), bf16[4096,1024]{1,0:T(8,128)(2,1)}) %all-gather.3.cloned.1.call-update) | async-done | bytes 8388624 | tf_op jit(solution)/shard_map/all_gather | solution.py:91
  74.6 3.2 %reduce-precision_convert_fusion = (bf16[4096,512]{1,0:T(8,128)(2,1)S(1)}, bf16[4096,512]{1,0:T(8,128)(2,1)S(1)}) fusion(f32[16,512]{1,0:T(8,128)S(1)} %broadcast_select_fusion, bf16[4096,1024]{1,0:T(8,128)(2,1)} %all-gather.3.cloned.1.call-done), kind=kLoop, calls=%fused_computation.1 | loop fusion | flops 12582912 | bytes 12615680 | tf_op jit(solution)/shard_map/convert_element_type | solution.py:108
  77.8 1.4 copy-done.1
  79.2 4.5 %fusion.1 = f32[512,1024]{1,0:T(8,128)S(1)} fusion(bf16[4096,512]{1,0:T(8,128)(2,1)S(1)} %get-tuple-element.11, bf16[4096,512]{1,0:T(8,128)(2,1)S(1)} %get-tuple-element.10, bf16[4096,1024]{1,0:T(8,128)(2,1)S(1)} %copy-done.1), kind=kOutput, calls=%fused_computation.3 | convolution fusion | flops 4311744512 | bytes 14680064 | tf_op jit(solution)/shard_map/dot_general | solution.py:110
  84.1 3.0 collective-permute-start.1
  87.1 1.8 collective-permute-start
  88.8 9.8 %collective-permute-done.1 = bf16[512,512]{1,0:T(8,128)(2,1)S(1)} collective-permute-done((bf16[512,512]{1,0:T(8,128)(2,1)S(1)}, bf16[512,512]{1,0:T(8,128)(2,1)S(1)}, u32[]{:S(2)}, u32[]{:S(2)}) %collective-permute-start.1) | collective-permute-done | bytes 524320 | tf_op jit(solution)/shard_map/ppermute | solution.py:122
  98.6 4.1 %collective-permute-done = bf16[512,512]{1,0:T(8,128)(2,1)S(1)} collective-permute-done((bf16[512,512]{1,0:T(8,128)(2,1)S(1)}, bf16[512,512]{1,0:T(8,128)(2,1)S(1)}, u32[]{:S(2)}, u32[]{:S(2)}) %collective-permute-start) | collective-permute-done | bytes 524320 | tf_op jit(solution)/shard_map/ppermute | solution.py:121
  104.2 1.9 fusion.59
  107.3 81.6 %all-reduce.2.cloned.1.call-done = f32[768,512]{0,1:T(8,128)} async-done(((f32[768,512]{0,1:T(8,128)}), f32[768,512]{0,1:T(8,128)}) %all-reduce.2.cloned.1.call-update) | async-done | bytes 1572880 | tf_op jit(solution)/shard_map/psum | solution.py:137
  190.9 11.7 %custom-call.12 = f32[128,128]{1,0:T(8,128)S(1)} custom-call(f32[128,128]{1,0:T(8,128)S(1)} %copy.45), custom_call_target="Cholesky" | custom-call | tf_op jit(solution)/shard_map/cholesky/custom-call.1 | solution.py:48
  204.0 9.8 %custom-call.13 = f32[1,128,128]{1,2,0:T(8,128)S(1)} custom-call(f32[1,128,128]{2,1,0:T(8,128)S(1)} %fusion.33), custom_call_target="InvertDiagBlocksLowerTriangular" | custom-call | tf_op jit(solution)/shard_map/triangular_solve/custom-call.0 | solution.py:49
  216.1 1.5 convolution_subtract_fusion.2
  218.6 1.5 convolution_subtract_fusion.5
  220.8 11.7 %custom-call.14 = f32[128,128]{1,0:T(8,128)S(1)} custom-call(f32[128,128]{1,0:T(8,128)S(1)} %copy.49), custom_call_target="Cholesky" | custom-call | tf_op jit(solution)/shard_map/cholesky/custom-call.1 | solution.py:48
  233.8 9.8 %custom-call.15 = f32[1,128,128]{1,2,0:T(8,128)S(1)} custom-call(f32[1,128,128]{2,1,0:T(8,128)S(1)} %fusion.34), custom_call_target="InvertDiagBlocksLowerTriangular" | custom-call | tf_op jit(solution)/shard_map/triangular_solve/custom-call.0 | solution.py:49
  248.7 11.7 %custom-call.16 = f32[128,128]{1,0:T(8,128)S(1)} custom-call(f32[128,128]{1,0:T(8,128)S(1)} %fusion.43), custom_call_target="Cholesky" | custom-call | tf_op jit(solution)/shard_map/cholesky/custom-call.1 | solution.py:48
  262.1 9.8 %custom-call.17 = f32[1,128,128]{1,2,0:T(8,128)S(1)} custom-call(f32[1,128,128]{2,1,0:T(8,128)S(1)} %fusion.35), custom_call_target="InvertDiagBlocksLowerTriangular" | custom-call | tf_op jit(solution)/shard_map/triangular_solve/custom-call.0 | solution.py:49
  273.3 1.4 convolution_subtract_fusion.8
  274.9 11.7 %custom-call.18 = f32[128,128]{1,0:T(8,128)S(1)} custom-call(f32[128,128]{1,0:T(8,128)S(1)} %broadcast_multiply_fusion), custom_call_target="Cholesky" | custom-call | tf_op jit(solution)/shard_map/cholesky/custom-call.1 | solution.py:48
  288.1 9.8 %custom-call.19 = f32[1,128,128]{1,2,0:T(8,128)S(1)} custom-call(f32[1,128,128]{2,1,0:T(8,128)S(1)} %fusion.36), custom_call_target="InvertDiagBlocksLowerTriangular" | custom-call | tf_op jit(solution)/shard_map/triangular_solve/custom-call.0 | solution.py:49
  298.2 1.3 fusion.60
  (91 shorter events, 27.3 us)
Async XLA Ops:
  7.2 67.4 %all-gather.3.cloned.1.call-start = ((), (), s32[]{:S(2)}) async-start(), calls=%async_computation | async-start | bytes 8912896 | tf_op jit(solution)/shard_map/all_gather | solution.py:91
  9.1 179.8 %all-reduce.2.cloned.1.call-start = ((), (), s32[]{:S(2)}) async-start(), calls=%async_computation.1 | async-start | bytes 3145728 | tf_op jit(solution)/shard_map/psum | solution.py:137
  74.6 4.7 %copy-start.1 = (bf16[4096,1024]{1,0:T(8,128)(2,1)S(1)}, bf16[4096,1024]{1,0:T(8,128)(2,1)}, u32[]{:S(2)}) copy-start(bf16[4096,1024]{1,0:T(8,128)(2,1)} %all-gather.3.cloned.1.call-done) | copy-start | bytes 25165828
  79.2 4.5 %copy-start.2 = (bf16[1,512,512]{2,1,0:T(8,128)(2,1)S(1)}, bf16[1,512,512]{2,1,0:T(8,128)(2,1)}, u32[]{:S(2)}) copy-start(bf16[1,512,512]{2,1,0:T(8,128)(2,1)} %param.10) | copy-start | bytes 1572868
  84.1 19.1 %copy-start.8 = (bf16[1,256,512]{2,1,0:T(8,128)(2,1)S(1)}, bf16[1,256,512]{2,1,0:T(8,128)(2,1)}, u32[]{:S(2)}) copy-start(bf16[1,256,512]{2,1,0:T(8,128)(2,1)} %param.7) | copy-start | bytes 786436
  84.1 14.5 %collective-permute-start.1 = (bf16[512,512]{1,0:T(8,128)(2,1)S(1)}, bf16[512,512]{1,0:T(8,128)(2,1)S(1)}, u32[]{:S(2)}, u32[]{:S(2)}) collective-permute-start(bf16[512,512]{1,0:T(8,128)(2,1)S(1)} %fusion.58), channel_id=1, source_target_pairs={{1,0},{2,1},{3,2},{5,4},{6,5},{7,6},{9,8},{10,9},{11,10},{13,12},{... | collective-permute-start | bytes 1572872 | tf_op jit(solution)/shard_map/ppermute | solution.py:122
  87.1 15.7 %collective-permute-start = (bf16[512,512]{1,0:T(8,128)(2,1)S(1)}, bf16[512,512]{1,0:T(8,128)(2,1)S(1)}, u32[]{:S(2)}, u32[]{:S(2)}) collective-permute-start(bf16[512,512]{1,0:T(8,128)(2,1)S(1)} %fusion.58), channel_id=1, source_target_pairs={{0,1},{1,2},{2,3},{4,5},{5,6},{6,7},{8,9},{9,10},{10,11},{12,13},{... | collective-permute-start | bytes 1572872 | tf_op jit(solution)/shard_map/ppermute | solution.py:121
  188.9 26.4 %slice-start.1 = ((f32[768,512]{0,1:T(8,128)}), f32[256,512]{0,1:T(8,128)S(1)}, s32[]{:S(2)}) async-start(f32[768,512]{0,1:T(8,128)} %all-reduce.2.cloned.1.call-done), calls=%async_computation.3 | async-start | bytes 1048576 | tf_op jit(solution)/shard_map/slice | solution.py:142
  215.3 4.8 %copy-start = (f32[384,128]{0,1:T(8,128)}, f32[384,128]{0,1:T(8,128)S(1)}, u32[]{:S(2)}) copy-start(f32[384,128]{0,1:T(8,128)S(1)} %fusion.17) | copy-start | bytes 589828
  217.6 2.5 copy-start.3
  220.5 23.2 %copy-start.7 = (f32[384,128]{0,1:T(8,128)}, f32[384,128]{0,1:T(8,128)S(1)}, u32[]{:S(2)}) copy-start(f32[384,128]{0,1:T(8,128)S(1)} %convolution_subtract_fusion.6) | copy-start | bytes 589828
  220.5 52.8 %slice-start = ((f32[384,128]{0,1:T(8,128)}), f32[128,128]{0,1:T(8,128)S(1)}, s32[]{:S(2)}) async-start(f32[384,128]{0,1:T(8,128)} %copy-done), calls=%async_computation.2 | async-start | bytes 131072 | tf_op jit(solution)/shard_map/slice | solution.py:67
  220.5 52.8 %copy-start.4 = (f32[768,512]{0,1:T(8,128)S(1)}, f32[768,512]{0,1:T(8,128)}, u32[]{:S(2)}) copy-start(f32[768,512]{0,1:T(8,128)} %all-reduce.2.cloned.1.call-done) | copy-start | bytes 4718596
  220.6 77.6 %copy-start.6 = (f32[768,128]{1,0:T(8,128)S(1)}, f32[768,128]{1,0:T(8,128)}, u32[]{:S(2)}) copy-start(f32[768,128]{1,0:T(8,128)} %convolution_subtract_fusion.5) | copy-start | bytes 1179652
  243.9 28.0 %copy-start.10 = (f32[128,128]{1,0:T(8,128)}, f32[128,128]{1,0:T(8,128)S(1)}, u32[]{:S(2)}) copy-start(f32[128,128]{1,0:T(8,128)S(1)} %convolution_select_fusion.2) | copy-start | bytes 196612
  244.0 55.6 %copy-start.5 = (f32[768,128]{1,0:T(8,128)S(1)}, f32[768,128]{1,0:T(8,128)}, u32[]{:S(2)}) copy-start(f32[768,128]{1,0:T(8,128)} %convolution_subtract_fusion.2) | copy-start | bytes 1179652
  247.1 0.7 copy-start.9
Sparse Core Ops, SparseCore 0:
  10.7 63.8 all-gather.2
  107.4 81.4 all-reduce.1

commit v3 on v2

--- a/solution.py
+++ b/solution.py
@@ -136,7 +136,7 @@
     )
     summed = lax.psum(jnp.concatenate([local_gram, local_proj], axis=0), "rx")
     gram = summed[:width]
-    block = 128
+    block = 64
     columns, inverses = blocked_factor(gram, block)
     solved = right_solve(
         jnp.concatenate([mixed, summed[width:]], axis=0), columns, inverses, block

time: 317 us -> 343 us (1.082)
  matrix products: 24.4 us -> 41.7 us
  other arithmetic: 101 us -> 105 us
    dot_general x6 -> x28, matrix products: 6.43 us -> 15.8 us  [right_solve(): jnp.dot(parts[k], col[top - c_top:top - c_top + block].T, precision=hi)]
    ppermute x1, waiting for transfers between devices: 9.77 us -> 1.18 us  [body(): above = lax.ppermute(sent, 'bin', downward).astype(jnp.float32)]
    dot_general x3 -> x7, matrix products: 3.06 us -> 8.99 us  [blocked_factor(): panel = panel - jnp.dot(done, done[:block].T, precision=hi)]
    ppermute x1, waiting for transfers between devices: 4.15 us -> 9.61 us  [body(): below = lax.ppermute(sent, 'bin', upward).astype(jnp.float32)]
    another operation x8 -> x16, other arithmetic: 41.9 us -> 44.5 us  [blocked_factor(): lax.linalg.triangular_solve(diag, eye, left_side=True, lower=True)]
    another operation x12 -> x24, other arithmetic: 49.9 us -> 52.5 us  [blocked_factor(): diag = lax.linalg.cholesky(panel[:block], symmetrize_input=True)]
where the time goes in v3:
time: 343 us; the launch traced here: 337 us
  waiting for transfers between devices  136 us (40%)
  other arithmetic  105 us (31%)
  matrix products  41.7 us (12%)
  blocking collectives  23.2 us (7%)
  between operations  15.3 us (4%)
  local copies, waits for them, and re-layouts  9.42 us (3%)
  starting transfers between devices  6.42 us (2%)
    psum x1, waiting for transfers between devices, body(): summed = lax.psum(jnp.concatenate([local_gram, local_proj], axis=0), 'rx')  83.5 us
    another operation x24, other arithmetic, blocked_factor(): diag = lax.linalg.cholesky(panel[:block], symmetrize_input=True)  52.5 us
    another operation x16, other arithmetic, blocked_factor(): lax.linalg.triangular_solve(diag, eye, left_side=True, lower=True)  44.5 us
    all_gather x1, waiting for transfers between devices, body(): lax.all_gather(jnp.concatenate([block_data, block_test], axis=1), 'tm', a...  41.6 us
    all_gather x1, blocking collectives, body(): decays = lax.all_gather(own_decay, 'tm', axis=0)  23.2 us
    dot_general x28, matrix products, right_solve(): jnp.dot(parts[k], col[top - c_top:top - c_top + block].T, precision=hi)  15.8 us
    ppermute x1, waiting for transfers between devices, body(): below = lax.ppermute(sent, 'bin', upward).astype(jnp.float32)  9.61 us
    dot_general x7, matrix products, blocked_factor(): panel = panel - jnp.dot(done, done[:block].T, precision=hi)  8.99 us
  transfers between devices with their start and end apart: 4, of which 4 were waited for; matrix products, arithmetic and copies ran while one was open for 0% of the time, Pallas kernels for 0%

profile of v3, /device:TPU:6, one launch (start us, length us, event | category | flops | bytes accessed | tf_op | source)
XLA Modules:
  0.0 337.1 jit_solution(10681635531064644622)
XLA Ops:
  7.2 1.9 pad_maximum_fusion.1
  9.2 23.2 %all-gather = f32[16,1,512]{2,1,0:T(1,128)S(1)} all-gather(f32[1,1,512]{2,1,0:T(1,128)S(1)} %copy-done.16), channel_id=2, replica_groups=mesh['rx'=8,'tm'=16,'bin'=4] {'tm'}, dimensions={0}, use_global_device_ids=true | all-gather | bytes 34816 | tf_op jit(solution)/shard_map/all_gather | solution.py:96
  33.1 41.6 %all-gather.3.cloned.1.call-done = bf16[4096,1024]{1,0:T(8,128)(2,1)} async-done(((bf16[256,1024]{1,0:T(8,128)(2,1)}), bf16[4096,1024]{1,0:T(8,128)(2,1)}) %all-gather.3.cloned.1.call-update) | async-done | bytes 8388624 | tf_op jit(solution)/shard_map/all_gather | solution.py:91
  74.7 3.1 reduce-precision_convert_fusion
  77.8 6.7 %fusion.1 = f32[512,1024]{0,1:T(8,128)S(1)} fusion(bf16[4096,512]{1,0:T(8,128)(2,1)S(1)} %get-tuple-element.13, bf16[4096,512]{1,0:T(8,128)(2,1)S(1)} %get-tuple-element.12, bf16[4096,1024]{1,0:T(8,128)(2,1)} %all-gather.3.cloned.1.call-done), kind=kOutput, calls=%fused_computation.3 | convolution fusion | flops 4311744512 | bytes 14680064 | tf_op jit(solution)/shard_map/dot_general | solution.py:110
  86.0 5.0 %collective-permute-start.1 = (bf16[512,512]{0,1:T(8,128)(2,1)S(1)}, bf16[512,512]{0,1:T(8,128)(2,1)S(1)}, u32[]{:S(2)}, u32[]{:S(2)}) collective-permute-start(bf16[512,512]{0,1:T(8,128)(2,1)S(1)} %fusion.130), channel_id=1, source_target_pairs={{1,0},{2,1},{3,2},{5,4},{6,5},{7,6},{9,8},{10,9},{11,10},{13,12},{... | collective-permute-start | bytes 1572872 | tf_op jit(solution)/shard_map/ppermute | solution.py:122
  91.1 9.6 %collective-permute-done = bf16[512,512]{0,1:T(8,128)(2,1)S(1)} collective-permute-done((bf16[512,512]{0,1:T(8,128)(2,1)S(1)}, bf16[512,512]{0,1:T(8,128)(2,1)S(1)}, u32[]{:S(2)}, u32[]{:S(2)}) %collective-permute-start) | collective-permute-done | bytes 524320 | tf_op jit(solution)/shard_map/ppermute | solution.py:121
  106.1 83.5 %all-reduce.2.cloned.1.call-done = f32[768,512]{0,1:T(8,128)} async-done(((f32[768,512]{0,1:T(8,128)}), f32[768,512]{0,1:T(8,128)}) %all-reduce.2.cloned.1.call-update) | async-done | bytes 1572880 | tf_op jit(solution)/shard_map/psum | solution.py:137
  191.2 5.9 %custom-call.20 = f32[64,64]{1,0:T(8,128)S(1)} custom-call(f32[64,64]{1,0:T(8,128)S(1)} %copy.125), custom_call_target="Cholesky" | custom-call | tf_op jit(solution)/shard_map/cholesky/custom-call.1 | solution.py:48
  198.4 4.9 %custom-call.21 = f32[1,64,64]{1,2,0:T(8,128)S(1)} custom-call(f32[1,64,64]{2,1,0:T(8,128)S(1)} %fusion.68), custom_call_target="InvertDiagBlocksLowerTriangular" | custom-call | tf_op jit(solution)/shard_map/triangular_solve/custom-call.0 | solution.py:49
  207.0 5.9 %custom-call.22 = f32[64,64]{1,0:T(8,128)S(1)} custom-call(f32[64,64]{1,0:T(8,128)S(1)} %copy.128), custom_call_target="Cholesky" | custom-call | tf_op jit(solution)/shard_map/cholesky/custom-call.1 | solution.py:48
  214.2 4.9 %custom-call.23 = f32[1,64,64]{1,2,0:T(8,128)S(1)} custom-call(f32[1,64,64]{2,1,0:T(8,128)S(1)} %fusion.69), custom_call_target="InvertDiagBlocksLowerTriangular" | custom-call | tf_op jit(solution)/shard_map/triangular_solve/custom-call.0 | solution.py:49
  232.8 5.9 %custom-call.24 = f32[64,64]{1,0:T(8,128)S(1)} custom-call(f32[64,64]{1,0:T(8,128)S(1)} %copy.131), custom_call_target="Cholesky" | custom-call | tf_op jit(solution)/shard_map/cholesky/custom-call.1 | solution.py:48
  240.1 4.9 %custom-call.25 = f32[1,64,64]{1,2,0:T(8,128)S(1)} custom-call(f32[1,64,64]{2,1,0:T(8,128)S(1)} %fusion.70), custom_call_target="InvertDiagBlocksLowerTriangular" | custom-call | tf_op jit(solution)/shard_map/triangular_solve/custom-call.0 | solution.py:49
  247.3 5.9 %custom-call.26 = f32[64,64]{1,0:T(8,128)S(1)} custom-call(f32[64,64]{1,0:T(8,128)S(1)} %copy.134), custom_call_target="Cholesky" | custom-call | tf_op jit(solution)/shard_map/cholesky/custom-call.1 | solution.py:48
  254.6 4.9 %custom-call.27 = f32[1,64,64]{1,2,0:T(8,128)S(1)} custom-call(f32[1,64,64]{2,1,0:T(8,128)S(1)} %fusion.71), custom_call_target="InvertDiagBlocksLowerTriangular" | custom-call | tf_op jit(solution)/shard_map/triangular_solve/custom-call.0 | solution.py:49
  261.7 5.9 %custom-call.28 = f32[64,64]{1,0:T(8,128)S(1)} custom-call(f32[64,64]{1,0:T(8,128)S(1)} %copy.137), custom_call_target="Cholesky" | custom-call | tf_op jit(solution)/shard_map/cholesky/custom-call.1 | solution.py:48
  269.0 4.9 %custom-call.29 = f32[1,64,64]{1,2,0:T(8,128)S(1)} custom-call(f32[1,64,64]{2,1,0:T(8,128)S(1)} %fusion.72), custom_call_target="InvertDiagBlocksLowerTriangular" | custom-call | tf_op jit(solution)/shard_map/triangular_solve/custom-call.0 | solution.py:49
  276.3 5.9 %custom-call.30 = f32[64,64]{1,0:T(8,128)S(1)} custom-call(f32[64,64]{1,0:T(8,128)S(1)} %copy.140), custom_call_target="Cholesky" | custom-call | tf_op jit(solution)/shard_map/cholesky/custom-call.1 | solution.py:48
  283.4 4.9 %custom-call.31 = f32[1,64,64]{1,2,0:T(8,128)S(1)} custom-call(f32[1,64,64]{2,1,0:T(8,128)S(1)} %fusion.73), custom_call_target="InvertDiagBlocksLowerTriangular" | custom-call | tf_op jit(solution)/shard_map/triangular_solve/custom-call.0 | solution.py:49
  290.2 5.8 %custom-call.32 = f32[64,64]{1,0:T(8,128)S(1)} custom-call(f32[64,64]{1,0:T(8,128)S(1)} %fusion.102), custom_call_target="Cholesky" | custom-call | tf_op jit(solution)/shard_map/cholesky/custom-call.1 | solution.py:48
  297.4 4.9 %custom-call.33 = f32[1,64,64]{1,2,0:T(8,128)S(1)} custom-call(f32[1,64,64]{2,1,0:T(8,128)S(1)} %fusion.74), custom_call_target="InvertDiagBlocksLowerTriangular" | custom-call | tf_op jit(solution)/shard_map/triangular_solve/custom-call.0 | solution.py:49
  304.6 5.9 %custom-call.34 = f32[64,64]{1,0:T(8,128)S(1)} custom-call(f32[64,64]{1,0:T(8,128)S(1)} %broadcast_multiply_fusion), custom_call_target="Cholesky" | custom-call | tf_op jit(solution)/shard_map/cholesky/custom-call.1 | solution.py:48
  311.8 5.1 %custom-call.35 = f32[1,64,64]{1,2,0:T(8,128)S(1)} custom-call(f32[1,64,64]{2,1,0:T(8,128)S(1)} %fusion.75), custom_call_target="InvertDiagBlocksLowerTriangular" | custom-call | tf_op jit(solution)/shard_map/triangular_solve/custom-call.0 | solution.py:49
  (194 shorter events, 61.0 us)
Async XLA Ops:
  7.2 2.1 copy-start.16
  7.2 25.3 %copy-start.11 = (bf16[1,512,512]{2,1,0:T(8,128)(2,1)S(1)}, bf16[1,512,512]{2,1,0:T(8,128)(2,1)}, u32[]{:S(2)}) copy-start(bf16[1,512,512]{2,1,0:T(8,128)(2,1)} %param.10) | copy-start | bytes 1572868
  7.2 67.5 %all-gather.3.cloned.1.call-start = ((), (), s32[]{:S(2)}) async-start(), calls=%async_computation | async-start | bytes 8912896 | tf_op jit(solution)/shard_map/all_gather | solution.py:91
  9.2 180.3 %all-reduce.2.cloned.1.call-start = ((), (), s32[]{:S(2)}) async-start(), calls=%async_computation.1 | async-start | bytes 3145728 | tf_op jit(solution)/shard_map/psum | solution.py:137
  84.7 16.0 %collective-permute-start = (bf16[512,512]{0,1:T(8,128)(2,1)S(1)}, bf16[512,512]{0,1:T(8,128)(2,1)S(1)}, u32[]{:S(2)}, u32[]{:S(2)}) collective-permute-start(bf16[512,512]{0,1:T(8,128)(2,1)S(1)} %fusion.130), channel_id=1, source_target_pairs={{0,1},{1,2},{2,3},{4,5},{5,6},{6,7},{8,9},{9,10},{10,11},{12,13},{... | collective-permute-start | bytes 1572872 | tf_op jit(solution)/shard_map/ppermute | solution.py:121
  86.0 15.8 %collective-permute-start.1 = (bf16[512,512]{0,1:T(8,128)(2,1)S(1)}, bf16[512,512]{0,1:T(8,128)(2,1)S(1)}, u32[]{:S(2)}, u32[]{:S(2)}) collective-permute-start(bf16[512,512]{0,1:T(8,128)(2,1)S(1)} %fusion.130), channel_id=1, source_target_pairs={{1,0},{2,1},{3,2},{5,4},{6,5},{7,6},{9,8},{10,9},{11,10},{13,12},{... | collective-permute-start | bytes 1572872 | tf_op jit(solution)/shard_map/ppermute | solution.py:122
  102.3 1.9 copy-start.1
  204.8 25.3 %copy-start = (f32[448,64]{0,1:T(8,128)}, f32[448,64]{0,1:T(8,128)S(1)}, u32[]{:S(2)}) copy-start(f32[448,64]{0,1:T(8,128)S(1)} %fusion.42) | copy-start | bytes 344068
  219.4 0.6 copy-start.12
  229.1 2.2 copy-start.3
  231.3 14.5 %slice-start = ((f32[448,64]{0,1:T(8,128)}), f32[320,64]{0,1:T(8,128)S(1)}, s32[]{:S(2)}) async-start(f32[448,64]{0,1:T(8,128)} %copy-done), calls=%async_computation.2 | async-start | bytes 196608 | tf_op jit(solution)/shard_map/slice | solution.py:46
  231.4 29.0 %copy-start.14 = (f32[256,64]{0,1:T(8,128)S(1)}, f32[256,64]{0,1:T(8,128)}, u32[]{:S(2)}) copy-start(f32[256,64]{0,1:T(8,128)} %slice.401) | copy-start | bytes 196612
  231.4 29.0 %copy-start.15 = (f32[256,64]{0,1:T(8,128)S(1)}, f32[256,64]{0,1:T(8,128)}, u32[]{:S(2)}) copy-start(f32[256,64]{0,1:T(8,128)} %slice.400) | copy-start | bytes 196612
  245.8 28.4 %copy-start.2 = (f32[128,384]{0,1:T(8,128)S(1)}, f32[128,384]{0,1:T(8,128)}, u32[]{:S(2)}) copy-start(f32[128,384]{0,1:T(8,128)} %constant_dynamic-update-slice_fusion.6) | copy-start | bytes 589828
  274.7 42.4 %copy-start.10 = (f32[768,64]{0,1:T(8,128)S(1)}, f32[768,64]{0,1:T(8,128)}, u32[]{:S(2)}) copy-start(f32[768,64]{0,1:T(8,128)} %convolution_subtract_fusion.27) | copy-start | bytes 589828
  274.7 42.4 %copy-start.13 = (f32[64,64]{1,0:T(8,128)S(1)}, f32[64,64]{1,0:T(8,128)}, u32[]{:S(2)}) copy-start(f32[64,64]{1,0:T(8,128)} %copy-done.12) | copy-start | bytes 49156
  276.2 41.3 %copy-start.8 = (f32[768,64]{0,1:T(8,128)S(1)}, f32[768,64]{0,1:T(8,128)}, u32[]{:S(2)}) copy-start(f32[768,64]{0,1:T(8,128)} %convolution_subtract_fusion.6) | copy-start | bytes 589828
  288.8 29.0 %copy-start.9 = (f32[768,64]{0,1:T(8,128)S(1)}, f32[768,64]{0,1:T(8,128)}, u32[]{:S(2)}) copy-start(f32[768,64]{0,1:T(8,128)} %convolution_subtract_fusion.26) | copy-start | bytes 589828
  302.6 15.7 %copy-start.7 = (f32[768,64]{0,1:T(8,128)S(1)}, f32[768,64]{0,1:T(8,128)}, u32[]{:S(2)}) copy-start(f32[768,64]{0,1:T(8,128)} %convolution_subtract_fusion.24) | copy-start | bytes 589828
  317.9 1.9 copy-start.6
  319.8 2.0 copy-start.5
  322.2 1.9 copy-start.4
Sparse Core Ops, SparseCore 0:
  10.7 63.9 all-gather.2
  106.2 83.2 all-reduce.1

commit v4 on v2

--- a/solution.py
+++ b/solution.py
@@ -32,6 +32,22 @@
     return block
 
 
+def lower_inverse(factor):
+    hi = lax.Precision.HIGHEST
+    size = factor.shape[0]
+    scale = jnp.diagonal(factor)
+    eye = jnp.eye(size, dtype=factor.dtype)
+    nil = eye - factor / scale[:, None]
+    power = nil
+    total = eye + nil
+    reach = 2
+    while reach < size:
+        power = jnp.dot(power, power, precision=hi)
+        total = total + jnp.dot(total, power, precision=hi)
+        reach *= 2
+    return jnp.tril(total / scale[None, :])
+
+
 def blocked_factor(gram, block):
     size = gram.shape[0]
     count = size // block
@@ -46,7 +62,7 @@
             done = jnp.concatenate([c[top - c_top:] for c_top, c in columns], axis=1)
             panel = panel - jnp.dot(done, done[:block].T, precision=hi)
         diag = lax.linalg.cholesky(panel[:block], symmetrize_input=True)
-        inverse = jnp.tril(lax.linalg.triangular_solve(diag, eye, left_side=True, lower=True))
+        inverse = lower_inverse(diag)
         inverses.append(inverse)
         if j + 1 < count:
             below = jnp.dot(panel[block:], inverse.T, precision=hi)

time: 317 us -> 286 us (0.902)
  other arithmetic: 101 us -> 60.9 us
  local copies, waits for them, and re-layouts: 6.48 us -> 11.7 us
  matrix products: 24.4 us -> 29 us
    another operation x8 -> x0, other arithmetic: 41.9 us -> none  [blocked_factor(): lax.linalg.triangular_solve(diag, eye, left_side=True, lower=True)]
    dot_general x0 -> x48, matrix products: none -> 10.3 us  [the longest x24 5.17 us: lower_inverse(): power = jnp.dot(power, power, precision=hi)]
    gather x0 -> x4, local copies, waits for them, and re-layouts: none -> 5.89 us  [lower_inverse(): scale = jnp.diagonal(factor)]
where the time goes in v4:
time: 286 us; the launch traced here: 282 us
  waiting for transfers between devices  137 us (48%)
  other arithmetic  60.9 us (21%)
  matrix products  29 us (10%)
  blocking collectives  23.5 us (8%)
  between operations  15.2 us (5%)
  local copies, waits for them, and re-layouts  11.7 us (4%)
  starting transfers between devices  4.65 us (2%)
    psum x1, waiting for transfers between devices, body(): summed = lax.psum(jnp.concatenate([local_gram, local_proj], axis=0), 'rx')  81.6 us
    another operation x12, other arithmetic, blocked_factor(): diag = lax.linalg.cholesky(panel[:block], symmetrize_input=True)  49.7 us
    all_gather x1, waiting for transfers between devices, body(): lax.all_gather(jnp.concatenate([block_data, block_test], axis=1), 'tm', a...  41.5 us
    all_gather x1, blocking collectives, body(): decays = lax.all_gather(own_decay, 'tm', axis=0)  23.5 us
    ppermute x1, waiting for transfers between devices, body(): above = lax.ppermute(sent, 'bin', downward).astype(jnp.float32)  9.94 us
    dot_general x6, matrix products, right_solve(): jnp.dot(parts[k], col[top - c_top:top - c_top + block].T, precision=hi)  6.26 us
    gather x4, local copies, waits for them, and re-layouts, lower_inverse(): scale = jnp.diagonal(factor)  5.89 us
  transfers between devices with their start and end apart: 4, of which 4 were waited for; matrix products, arithmetic and copies ran while one was open for 0% of the time, Pallas kernels for 0%

profile of v4, /device:TPU:6, one launch (start us, length us, event | category | flops | bytes accessed | tf_op | source)
XLA Modules:
  0.0 282.2 jit_solution(13589947021889970446)
XLA Ops:
  7.2 1.9 pad_maximum_fusion.2
  9.2 23.5 %all-gather = f32[16,1,512]{2,1,0:T(1,128)S(1)} all-gather(f32[1,1,512]{2,1,0:T(1,128)} %param.7), channel_id=2, replica_groups=mesh['rx'=8,'tm'=16,'bin'=4] {'tm'}, dimensions={0}, use_global_device_ids=true | all-gather | bytes 34816 | tf_op jit(solution)/shard_map/all_gather | solution.py:112
  33.0 41.5 %all-gather.3.cloned.1.call-done = bf16[4096,1024]{1,0:T(8,128)(2,1)} async-done(((bf16[256,1024]{1,0:T(8,128)(2,1)}), bf16[4096,1024]{1,0:T(8,128)(2,1)}) %all-gather.3.cloned.1.call-update) | async-done | bytes 8388624 | tf_op jit(solution)/shard_map/all_gather | solution.py:107
  74.6 3.2 %reduce-precision_convert_fusion = (bf16[4096,512]{1,0:T(8,128)(2,1)S(1)}, bf16[4096,512]{1,0:T(8,128)(2,1)S(1)}) fusion(f32[16,512]{1,0:T(8,128)S(1)} %broadcast_select_fusion, bf16[4096,1024]{1,0:T(8,128)(2,1)} %all-gather.3.cloned.1.call-done), kind=kLoop, calls=%fused_computation.5 | loop fusion | flops 12582912 | bytes 12615680 | tf_op jit(solution)/shard_map/convert_element_type | solution.py:124
  77.8 1.4 copy-done.1
  79.2 4.5 %fusion.1 = f32[512,1024]{1,0:T(8,128)S(1)} fusion(bf16[4096,512]{1,0:T(8,128)(2,1)S(1)} %get-tuple-element.12, bf16[4096,512]{1,0:T(8,128)(2,1)S(1)} %get-tuple-element.11, bf16[4096,1024]{1,0:T(8,128)(2,1)S(1)} %copy-done.1), kind=kOutput, calls=%fused_computation.7 | convolution fusion | flops 4311744512 | bytes 14680064 | tf_op jit(solution)/shard_map/dot_general | solution.py:126
  84.1 3.0 %collective-permute-start.1 = (bf16[512,512]{1,0:T(8,128)(2,1)S(1)}, bf16[512,512]{1,0:T(8,128)(2,1)S(1)}, u32[]{:S(2)}, u32[]{:S(2)}) collective-permute-start(bf16[512,512]{1,0:T(8,128)(2,1)S(1)} %fusion.58), channel_id=1, source_target_pairs={{1,0},{2,1},{3,2},{5,4},{6,5},{7,6},{9,8},{10,9},{11,10},{13,12},{... | collective-permute-start | bytes 1572872 | tf_op jit(solution)/shard_map/ppermute | solution.py:138
  87.1 1.6 collective-permute-start
  88.7 9.9 %collective-permute-done.1 = bf16[512,512]{1,0:T(8,128)(2,1)S(1)} collective-permute-done((bf16[512,512]{1,0:T(8,128)(2,1)S(1)}, bf16[512,512]{1,0:T(8,128)(2,1)S(1)}, u32[]{:S(2)}, u32[]{:S(2)}) %collective-permute-start.1) | collective-permute-done | bytes 524320 | tf_op jit(solution)/shard_map/ppermute | solution.py:138
  98.6 4.1 %collective-permute-done = bf16[512,512]{1,0:T(8,128)(2,1)S(1)} collective-permute-done((bf16[512,512]{1,0:T(8,128)(2,1)S(1)}, bf16[512,512]{1,0:T(8,128)(2,1)S(1)}, u32[]{:S(2)}, u32[]{:S(2)}) %collective-permute-start) | collective-permute-done | bytes 524320 | tf_op jit(solution)/shard_map/ppermute | solution.py:137
  104.2 1.9 fusion.59
  106.1 1.2 pad_maximum_fusion
  107.4 81.6 %all-reduce.2.cloned.1.call-done = f32[768,512]{0,1:T(8,128)} async-done(((f32[768,512]{0,1:T(8,128)}), f32[768,512]{0,1:T(8,128)}) %all-reduce.2.cloned.1.call-update) | async-done | bytes 1572880 | tf_op jit(solution)/shard_map/psum | solution.py:153
  190.9 11.7 %custom-call.14 = f32[128,128]{1,0:T(8,128)S(1)} custom-call(f32[128,128]{1,0:T(8,128)S(1)} %copy.62), custom_call_target="Cholesky" | custom-call | tf_op jit(solution)/shard_map/cholesky/custom-call.1 | solution.py:64
  203.9 1.8 gather_fusion
  210.9 1.5 convolution_subtract_fusion.5
  213.1 11.7 %custom-call.15 = f32[128,128]{1,0:T(8,128)S(1)} custom-call(f32[128,128]{1,0:T(8,128)S(1)} %copy.66), custom_call_target="Cholesky" | custom-call | tf_op jit(solution)/shard_map/cholesky/custom-call.1 | solution.py:64
  226.1 1.4 gather_fusion.1
  228.3 1.5 convolution_subtract_fusion.4
  232.6 11.7 %custom-call.16 = f32[128,128]{1,0:T(8,128)S(1)} custom-call(f32[128,128]{1,0:T(8,128)S(1)} %fusion.41), custom_call_target="Cholesky" | custom-call | tf_op jit(solution)/shard_map/cholesky/custom-call.1 | solution.py:64
  245.7 1.5 gather_fusion.2
  250.8 11.7 %custom-call.17 = f32[128,128]{1,0:T(8,128)S(1)} custom-call(f32[128,128]{1,0:T(8,128)S(1)} %broadcast_multiply_fusion), custom_call_target="Cholesky" | custom-call | tf_op jit(solution)/shard_map/cholesky/custom-call.1 | solution.py:64
  264.0 1.2 gather_fusion.3
  266.0 1.5 fusion.70
  (131 shorter events, 30.2 us)
Async XLA Ops:
  7.2 67.4 %all-gather.3.cloned.1.call-start = ((), (), s32[]{:S(2)}) async-start(), calls=%async_computation | async-start | bytes 8912896 | tf_op jit(solution)/shard_map/all_gather | solution.py:107
  9.1 179.9 %all-reduce.2.cloned.1.call-start = ((), (), s32[]{:S(2)}) async-start(), calls=%async_computation.1 | async-start | bytes 3145728 | tf_op jit(solution)/shard_map/psum | solution.py:153
  74.6 4.7 %copy-start.1 = (bf16[4096,1024]{1,0:T(8,128)(2,1)S(1)}, bf16[4096,1024]{1,0:T(8,128)(2,1)}, u32[]{:S(2)}) copy-start(bf16[4096,1024]{1,0:T(8,128)(2,1)} %all-gather.3.cloned.1.call-done) | copy-start | bytes 25165828
  79.2 4.5 %copy-start.2 = (bf16[1,512,512]{2,1,0:T(8,128)(2,1)S(1)}, bf16[1,512,512]{2,1,0:T(8,128)(2,1)}, u32[]{:S(2)}) copy-start(bf16[1,512,512]{2,1,0:T(8,128)(2,1)} %param.8) | copy-start | bytes 1572868
  84.1 19.1 %copy-start.7 = (bf16[1,256,512]{2,1,0:T(8,128)(2,1)S(1)}, bf16[1,256,512]{2,1,0:T(8,128)(2,1)}, u32[]{:S(2)}) copy-start(bf16[1,256,512]{2,1,0:T(8,128)(2,1)} %param.5) | copy-start | bytes 786436
  84.1 14.5 %collective-permute-start.1 = (bf16[512,512]{1,0:T(8,128)(2,1)S(1)}, bf16[512,512]{1,0:T(8,128)(2,1)S(1)}, u32[]{:S(2)}, u32[]{:S(2)}) collective-permute-start(bf16[512,512]{1,0:T(8,128)(2,1)S(1)} %fusion.58), channel_id=1, source_target_pairs={{1,0},{2,1},{3,2},{5,4},{6,5},{7,6},{9,8},{10,9},{11,10},{13,12},{... | collective-permute-start | bytes 1572872 | tf_op jit(solution)/shard_map/ppermute | solution.py:138
  87.1 15.7 %collective-permute-start = (bf16[512,512]{1,0:T(8,128)(2,1)S(1)}, bf16[512,512]{1,0:T(8,128)(2,1)S(1)}, u32[]{:S(2)}, u32[]{:S(2)}) collective-permute-start(bf16[512,512]{1,0:T(8,128)(2,1)S(1)} %fusion.58), channel_id=1, source_target_pairs={{0,1},{1,2},{2,3},{4,5},{5,6},{6,7},{8,9},{9,10},{10,11},{12,13},{... | collective-permute-start | bytes 1572872 | tf_op jit(solution)/shard_map/ppermute | solution.py:137
  190.9 17.3 %slice-start.2 = ((f32[768,512]{0,1:T(8,128)}), f32[256,512]{0,1:T(8,128)S(1)}, s32[]{:S(2)}) async-start(f32[768,512]{0,1:T(8,128)} %all-reduce.2.cloned.1.call-done), calls=%async_computation.4 | async-start | bytes 1048576 | tf_op jit(solution)/shard_map/slice | solution.py:158
  208.4 1.4 copy-start.3
  210.1 19.8 %copy-start = (f32[384,128]{0,1:T(8,128)}, f32[384,128]{0,1:T(8,128)S(1)}, u32[]{:S(2)}) copy-start(f32[384,128]{0,1:T(8,128)S(1)} %fusion.25) | copy-start | bytes 589828
  228.3 3.7 %copy-start.4 = (f32[768,512]{0,1:T(8,128)S(1)}, f32[768,512]{0,1:T(8,128)}, u32[]{:S(2)}) copy-start(f32[768,512]{0,1:T(8,128)} %all-reduce.2.cloned.1.call-done) | copy-start | bytes 4718596
  229.9 2.2 slice-start
  232.5 17.6 %slice-start.1 = ((f32[384,128]{0,1:T(8,128)}), f32[128,128]{0,1:T(8,128)S(1)}, s32[]{:S(2)}) async-start(f32[384,128]{0,1:T(8,128)} %copy-done), calls=%async_computation.3 | async-start | bytes 131072 | tf_op jit(solution)/shard_map/slice | solution.py:83
  232.5 17.6 %copy-start.5 = (f32[768,512]{0,1:T(8,128)S(1)}, f32[768,512]{0,1:T(8,128)}, u32[]{:S(2)}) copy-start(f32[768,512]{0,1:T(8,128)} %all-reduce.2.cloned.1.call-done) | copy-start | bytes 4718596
  250.6 17.7 %copy-start.6 = (f32[768,128]{1,0:T(8,128)S(1)}, f32[768,128]{1,0:T(8,128)}, u32[]{:S(2)}) copy-start(f32[768,128]{1,0:T(8,128)} %convolution_subtract_fusion.4) | copy-start | bytes 1179652
Sparse Core Ops, SparseCore 0:
  10.7 63.8 all-gather.2
  107.5 81.4 all-reduce.1

commit v5 on v4

--- a/solution.py
+++ b/solution.py
@@ -35,8 +35,8 @@
 def lower_inverse(factor):
     hi = lax.Precision.HIGHEST
     size = factor.shape[0]
-    scale = jnp.diagonal(factor)
     eye = jnp.eye(size, dtype=factor.dtype)
+    scale = jnp.sum(factor * eye, axis=1)
     nil = eye - factor / scale[:, None]
     power = nil
     total = eye + nil
@@ -61,7 +61,7 @@
         if j:
             done = jnp.concatenate([c[top - c_top:] for c_top, c in columns], axis=1)
             panel = panel - jnp.dot(done, done[:block].T, precision=hi)
-        diag = lax.linalg.cholesky(panel[:block], symmetrize_input=True)
+        diag = lax.linalg.cholesky(panel[:block], symmetrize_input=False)
         inverse = lower_inverse(diag)
         inverses.append(inverse)
         if j + 1 < count:

time: 286 us -> 281 us (0.983)
  local copies, waits for them, and re-layouts: 11.7 us -> 4.48 us
    gather x4 -> x0, local copies, waits for them, and re-layouts: 5.89 us -> none  [lower_inverse(): scale = jnp.diagonal(factor)]
    reduce_sum x0 -> x4, other arithmetic: none -> 2.99 us  [lower_inverse(): scale = jnp.sum(factor * eye, axis=1)]
where the time goes in v5:
time: 281 us; the launch traced here: 277 us
  waiting for transfers between devices  137 us (49%)
  other arithmetic  60.5 us (22%)
  matrix products  31.8 us (11%)
  blocking collectives  23.5 us (8%)
  between operations  15 us (5%)
  starting transfers between devices  4.82 us (2%)
  local copies, waits for them, and re-layouts  4.48 us (2%)
    psum x1, waiting for transfers between devices, body(): summed = lax.psum(jnp.concatenate([local_gram, local_proj], axis=0), 'rx')  81.6 us
    another operation x12, other arithmetic, blocked_factor(): diag = lax.linalg.cholesky(panel[:block], symmetrize_input=False)  49.9 us
    all_gather x1, waiting for transfers between devices, body(): lax.all_gather(jnp.concatenate([block_data, block_test], axis=1), 'tm', a...  41.5 us
    all_gather x1, blocking collectives, body(): decays = lax.all_gather(own_decay, 'tm', axis=0)  23.5 us
    ppermute x1, waiting for transfers between devices, body(): above = lax.ppermute(sent, 'bin', downward).astype(jnp.float32)  9.77 us
    dot_general x24, matrix products, lower_inverse(): power = jnp.dot(power, power, precision=hi)  7.78 us
    dot_general x24, matrix products, lower_inverse(): total = total + jnp.dot(total, power, precision=hi)  7.74 us
  transfers between devices with their start and end apart: 4, of which 4 were waited for; matrix products, arithmetic and copies ran while one was open for 0% of the time, Pallas kernels for 0%

profile of v5, /device:TPU:6, one launch (start us, length us, event | category | flops | bytes accessed | tf_op | source)
XLA Modules:
  0.0 277.2 jit_solution(3977654754126049880)
XLA Ops:
  7.2 1.9 pad_maximum_fusion.2
  9.2 23.5 %all-gather = f32[16,1,512]{2,1,0:T(1,128)S(1)} all-gather(f32[1,1,512]{2,1,0:T(1,128)} %param.7), channel_id=2, replica_groups=mesh['rx'=8,'tm'=16,'bin'=4] {'tm'}, dimensions={0}, use_global_device_ids=true | all-gather | bytes 34816 | tf_op jit(solution)/shard_map/all_gather | solution.py:112
  33.0 41.5 %all-gather.3.cloned.1.call-done = bf16[4096,1024]{1,0:T(8,128)(2,1)} async-done(((bf16[256,1024]{1,0:T(8,128)(2,1)}), bf16[4096,1024]{1,0:T(8,128)(2,1)}) %all-gather.3.cloned.1.call-update) | async-done | bytes 8388624 | tf_op jit(solution)/shard_map/all_gather | solution.py:107
  74.6 3.2 %reduce-precision_convert_fusion = (bf16[4096,512]{1,0:T(8,128)(2,1)S(1)}, bf16[4096,512]{1,0:T(8,128)(2,1)S(1)}) fusion(f32[16,512]{1,0:T(8,128)S(1)} %broadcast_select_fusion, bf16[4096,1024]{1,0:T(8,128)(2,1)} %all-gather.3.cloned.1.call-done), kind=kLoop, calls=%fused_computation.1 | loop fusion | flops 12582912 | bytes 12615680 | tf_op jit(solution)/shard_map/convert_element_type | solution.py:124
  77.8 1.4 copy-done.2
  79.2 4.5 %fusion.1 = f32[512,1024]{1,0:T(8,128)S(1)} fusion(bf16[4096,512]{1,0:T(8,128)(2,1)S(1)} %get-tuple-element.10, bf16[4096,512]{1,0:T(8,128)(2,1)S(1)} %get-tuple-element.9, bf16[4096,1024]{1,0:T(8,128)(2,1)S(1)} %copy-done.2), kind=kOutput, calls=%fused_computation.3 | convolution fusion | flops 4311744512 | bytes 14680064 | tf_op jit(solution)/shard_map/dot_general | solution.py:126
  84.1 3.0 %collective-permute-start.1 = (bf16[512,512]{1,0:T(8,128)(2,1)S(1)}, bf16[512,512]{1,0:T(8,128)(2,1)S(1)}, u32[]{:S(2)}, u32[]{:S(2)}) collective-permute-start(bf16[512,512]{1,0:T(8,128)(2,1)S(1)} %fusion.55), channel_id=1, source_target_pairs={{1,0},{2,1},{3,2},{5,4},{6,5},{7,6},{9,8},{10,9},{11,10},{13,12},{... | collective-permute-start | bytes 1572872 | tf_op jit(solution)/shard_map/ppermute | solution.py:138
  87.1 1.8 collective-permute-start
  88.8 9.8 %collective-permute-done.1 = bf16[512,512]{1,0:T(8,128)(2,1)S(1)} collective-permute-done((bf16[512,512]{1,0:T(8,128)(2,1)S(1)}, bf16[512,512]{1,0:T(8,128)(2,1)S(1)}, u32[]{:S(2)}, u32[]{:S(2)}) %collective-permute-start.1) | collective-permute-done | bytes 524320 | tf_op jit(solution)/shard_map/ppermute | solution.py:138
  98.6 4.1 %collective-permute-done = bf16[512,512]{1,0:T(8,128)(2,1)S(1)} collective-permute-done((bf16[512,512]{1,0:T(8,128)(2,1)S(1)}, bf16[512,512]{1,0:T(8,128)(2,1)S(1)}, u32[]{:S(2)}, u32[]{:S(2)}) %collective-permute-start) | collective-permute-done | bytes 524320 | tf_op jit(solution)/shard_map/ppermute | solution.py:137
  103.8 1.9 fusion.56
  105.7 1.3 pad_maximum_fusion
  107.0 81.6 %all-reduce.2.cloned.1.call-done = f32[768,512]{1,0:T(8,128)} async-done(((f32[768,512]{1,0:T(8,128)}), f32[768,512]{1,0:T(8,128)}) %all-reduce.2.cloned.1.call-update) | async-done | bytes 1572880 | tf_op jit(solution)/shard_map/psum | solution.py:153
  188.6 1.0 slice.133
  189.5 11.7 %custom-call.6 = f32[128,128]{1,0:T(8,128)S(1)} custom-call(f32[128,128]{1,0:T(8,128)S(1)} %slice.133), custom_call_target="Cholesky" | custom-call | tf_op jit(solution)/shard_map/cholesky/custom-call.1 | solution.py:64
  202.7 0.9 fusion.51
  207.6 11.9 %custom-call.7 = f32[128,128]{1,0:T(8,128)S(1)} custom-call(f32[128,128]{1,0:T(8,128)S(1)} %slice.139), custom_call_target="Cholesky" | custom-call | tf_op jit(solution)/shard_map/cholesky/custom-call.1 | solution.py:64
  220.9 0.9 fusion.52
  225.8 11.7 %custom-call.8 = f32[128,128]{1,0:T(8,128)S(1)} custom-call(f32[128,128]{1,0:T(8,128)S(1)} %slice.147), custom_call_target="Cholesky" | custom-call | tf_op jit(solution)/shard_map/cholesky/custom-call.1 | solution.py:64
  238.9 0.9 fusion.53
  243.7 11.9 %custom-call.9 = f32[128,128]{1,0:T(8,128)S(1)} custom-call(f32[128,128]{1,0:T(8,128)S(1)} %convolution_subtract_fusion.8), custom_call_target="Cholesky" | custom-call | tf_op jit(solution)/shard_map/cholesky/custom-call.1 | solution.py:64
  257.0 0.9 fusion.54
  268.1 1.0 copy.10
  269.1 1.0 copy.11
  (107 shorter events, 28.9 us)
Async XLA Ops:
  7.2 67.4 %all-gather.3.cloned.1.call-start = ((), (), s32[]{:S(2)}) async-start(), calls=%async_computation | async-start | bytes 8912896 | tf_op jit(solution)/shard_map/all_gather | solution.py:107
  9.1 179.5 %all-reduce.2.cloned.1.call-start = ((), (), s32[]{:S(2)}) async-start(), calls=%async_computation.1 | async-start | bytes 3145728 | tf_op jit(solution)/shard_map/psum | solution.py:153
  74.6 4.7 %copy-start.2 = (bf16[4096,1024]{1,0:T(8,128)(2,1)S(1)}, bf16[4096,1024]{1,0:T(8,128)(2,1)}, u32[]{:S(2)}) copy-start(bf16[4096,1024]{1,0:T(8,128)(2,1)} %all-gather.3.cloned.1.call-done) | copy-start | bytes 25165828
  79.2 4.5 %copy-start.3 = (bf16[1,512,512]{2,1,0:T(8,128)(2,1)S(1)}, bf16[1,512,512]{2,1,0:T(8,128)(2,1)}, u32[]{:S(2)}) copy-start(bf16[1,512,512]{2,1,0:T(8,128)(2,1)} %param.8) | copy-start | bytes 1572868
  84.1 19.1 %copy-start.4 = (bf16[1,256,512]{2,1,0:T(8,128)(2,1)S(1)}, bf16[1,256,512]{2,1,0:T(8,128)(2,1)}, u32[]{:S(2)}) copy-start(bf16[1,256,512]{2,1,0:T(8,128)(2,1)} %param.5) | copy-start | bytes 786436
  84.1 14.5 %collective-permute-start.1 = (bf16[512,512]{1,0:T(8,128)(2,1)S(1)}, bf16[512,512]{1,0:T(8,128)(2,1)S(1)}, u32[]{:S(2)}, u32[]{:S(2)}) collective-permute-start(bf16[512,512]{1,0:T(8,128)(2,1)S(1)} %fusion.55), channel_id=1, source_target_pairs={{1,0},{2,1},{3,2},{5,4},{6,5},{7,6},{9,8},{10,9},{11,10},{13,12},{... | collective-permute-start | bytes 1572872 | tf_op jit(solution)/shard_map/ppermute | solution.py:138
  87.1 15.7 %collective-permute-start = (bf16[512,512]{1,0:T(8,128)(2,1)S(1)}, bf16[512,512]{1,0:T(8,128)(2,1)S(1)}, u32[]{:S(2)}, u32[]{:S(2)}) collective-permute-start(bf16[512,512]{1,0:T(8,128)(2,1)S(1)} %fusion.55), channel_id=1, source_target_pairs={{0,1},{1,2},{2,3},{4,5},{5,6},{6,7},{8,9},{9,10},{10,11},{12,13},{... | collective-permute-start | bytes 1572872 | tf_op jit(solution)/shard_map/ppermute | solution.py:137
  188.6 18.1 %copy-start.5 = (f32[768,512]{1,0:T(8,128)S(1)}, f32[768,512]{1,0:T(8,128)}, u32[]{:S(2)}) copy-start(f32[768,512]{1,0:T(8,128)} %all-reduce.2.cloned.1.call-done) | copy-start | bytes 4718596
  207.1 18.1 %copy-start = (f32[384,128]{0,1:T(8,128)}, f32[384,128]{0,1:T(8,128)S(1)}, u32[]{:S(2)}) copy-start(f32[384,128]{0,1:T(8,128)S(1)} %fusion.25) | copy-start | bytes 589828
  225.8 17.4 %slice-start = ((f32[384,128]{0,1:T(8,128)}), f32[128,128]{0,1:T(8,128)S(1)}, s32[]{:S(2)}) async-start(f32[384,128]{0,1:T(8,128)} %copy-done), calls=%async_computation.2 | async-start | bytes 131072 | tf_op jit(solution)/shard_map/slice | solution.py:83
  243.7 16.0 %copy-start.1 = (f32[384,128]{0,1:T(8,128)S(1)}, f32[384,128]{0,1:T(8,128)}, u32[]{:S(2)}) copy-start(f32[384,128]{0,1:T(8,128)} %copy-done) | copy-start | bytes 589828
Sparse Core Ops, SparseCore 0:
  10.7 63.8 all-gather.2
  107.1 81.4 all-reduce.1

commit v6 on v5

--- a/solution.py
+++ b/solution.py
@@ -104,11 +104,7 @@
     rows = block_data.shape[1]
     steps = lax.axis_size("tm")
     place = lax.axis_index("tm")
-    gathered = lax.all_gather(
-        jnp.concatenate([block_data, block_test], axis=1), "tm", axis=0, tiled=True
-    )
-    all_data = gathered[:, :rows]
-    all_test = gathered[:, rows:]
+    all_data, all_test = lax.all_gather((block_data, block_test), "tm", axis=0, tiled=True)
     decays = lax.all_gather(own_decay, "tm", axis=0)
     owner = lax.broadcasted_iota(jnp.int32, (steps, steps, 1), 0)
     later = lax.broadcasted_iota(jnp.int32, (steps, steps, 1), 1)

time: 281 us -> 314 us (1.12)
  waiting for transfers between devices: 137 us -> 162 us
  matrix products: 31.8 us -> 36.5 us
    all_gather x1 -> x2, waiting for transfers between devices: 41.5 us -> 65.7 us  [body(): lax.all_gather((block_data, block_test), 'tm', axis=0, tiled=True)]
    ppermute x1, waiting for transfers between devices: 9.77 us -> 1.18 us  [body(): above = lax.ppermute(sent, 'bin', downward).astype(jnp.float32)]
    ppermute x1, waiting for transfers between devices: 4.15 us -> 9.6 us  [body(): below = lax.ppermute(sent, 'bin', upward).astype(jnp.float32)]
    dot_general x1, matrix products: 4.5 us -> 9.21 us  [body(): lax.dot_general(all_data, jnp.concatenate([high, low], axis=1), (((0,), (...]
    convert_element_type x1, other arithmetic: 3.25 us -> 6.89 us  [body(): high = rounded.astype(jnp.bfloat16)]
  transfers between devices with their start and end apart: 4 -> 5, of which waited for: 4 -> 5; matrix products, arithmetic and copies ran while one was open for 0% -> 2% of each run, Pallas kernels for 0% -> 0%
where the time goes in v6:
time: 314 us; the launch traced here: 308 us
  waiting for transfers between devices  162 us (52%)
  other arithmetic  62.3 us (20%)
  matrix products  36.5 us (12%)
  blocking collectives  23.5 us (7%)
  between operations  14.7 us (5%)
  starting transfers between devices  6.45 us (2%)
    psum x1, waiting for transfers between devices, body(): summed = lax.psum(jnp.concatenate([local_gram, local_proj], axis=0), 'rx')  83.8 us
    all_gather x2, waiting for transfers between devices, body(): lax.all_gather((block_data, block_test), 'tm', axis=0, tiled=True)  65.7 us
    another operation x12, other arithmetic, blocked_factor(): diag = lax.linalg.cholesky(panel[:block], symmetrize_input=False)  49.9 us
    all_gather x1, blocking collectives, body(): decays = lax.all_gather(own_decay, 'tm', axis=0)  23.5 us
    ppermute x1, waiting for transfers between devices, body(): below = lax.ppermute(sent, 'bin', upward).astype(jnp.float32)  9.6 us
    dot_general x1, matrix products, body(): lax.dot_general(all_data, jnp.concatenate([high, low], axis=1), (((0,), (...  9.21 us
    dot_general x24, matrix products, lower_inverse(): power = jnp.dot(power, power, precision=hi)  7.79 us
    dot_general x24, matrix products, lower_inverse(): total = total + jnp.dot(total, power, precision=hi)  7.74 us
  transfers between devices with their start and end apart: 5, of which 5 were waited for; matrix products, arithmetic and copies ran while one was open for 2% of the time, Pallas kernels for 0%

profile of v6, /device:TPU:6, one launch (start us, length us, event | category | flops | bytes accessed | tf_op | source)
XLA Modules:
  0.0 308.2 jit_solution(528381534868333646)
XLA Ops:
  8.7 23.5 %all-gather.1 = f32[16,1,512]{2,1,0:T(1,128)S(1)} all-gather(f32[1,1,512]{2,1,0:T(1,128)} %param.7), channel_id=3, replica_groups=mesh['rx'=8,'tm'=16,'bin'=4] {'tm'}, dimensions={0}, use_global_device_ids=true | all-gather | bytes 34816 | tf_op jit(solution)/shard_map/all_gather | solution.py:108
  32.6 27.6 %all-gather.6.cloned.1.call-done = bf16[1,4096,512]{2,1,0:T(8,128)(2,1)} async-done(((bf16[1,256,512]{2,1,0:T(8,128)(2,1)}), bf16[1,4096,512]{2,1,0:T(8,128)(2,1)}) %all-gather.6.cloned.1.call-update) | async-done | bytes 4194320 | tf_op jit(solution)/shard_map/all_gather | solution.py:107
  60.1 6.9 %reduce-precision_convert_fusion = (bf16[4096,512]{1,0:T(8,128)(2,1)}, bf16[4096,512]{1,0:T(8,128)(2,1)}) fusion(bf16[1,4096,512]{2,1,0:T(8,128)(2,1)} %all-gather.6.cloned.1.call-done, f32[16,512]{1,0:T(8,128)S(1)} %broadcast_select_fusion), kind=kLoop, calls=%fused_computation.1 | loop fusion | flops 12582912 | bytes 12615680 | tf_op jit(solution)/shard_map/convert_element_type | solution.py:120
  67.0 38.2 %all-gather.8.cloned.1.call-done = bf16[1,4096,512]{2,1,0:T(8,128)(2,1)} async-done(((bf16[1,256,512]{2,1,0:T(8,128)(2,1)}), bf16[1,4096,512]{2,1,0:T(8,128)(2,1)}) %all-gather.8.cloned.1.call-update) | async-done | bytes 4194320 | tf_op jit(solution)/shard_map/all_gather | solution.py:107
  105.2 9.2 %fusion.6 = f32[512,1024]{1,0:T(8,128)S(1)} fusion(bf16[1,4096,512]{2,1,0:T(8,128)(2,1)} %all-gather.8.cloned.1.call-done, bf16[4096,512]{1,0:T(8,128)(2,1)} %get-tuple-element.10, bf16[4096,512]{1,0:T(8,128)(2,1)} %get-tuple-element.9), kind=kOutput, calls=%fused_computation.15 | convolution fusion | flops 4311744512 | bytes 14680064 | tf_op jit(solution)/shard_map/dot_general | solution.py:122
  114.7 1.3 collective-permute-start
  116.0 5.0 %collective-permute-start.1 = (bf16[512,512]{1,0:T(8,128)(2,1)S(1)}, bf16[512,512]{1,0:T(8,128)(2,1)S(1)}, u32[]{:S(2)}, u32[]{:S(2)}) collective-permute-start(bf16[512,512]{1,0:T(8,128)(2,1)S(1)} %fusion.60), channel_id=1, source_target_pairs={{1,0},{2,1},{3,2},{5,4},{6,5},{7,6},{9,8},{10,9},{11,10},{13,12},{... | collective-permute-start | bytes 1572872 | tf_op jit(solution)/shard_map/ppermute | solution.py:134
  121.1 9.6 %collective-permute-done = bf16[512,512]{1,0:T(8,128)(2,1)S(1)} collective-permute-done((bf16[512,512]{1,0:T(8,128)(2,1)S(1)}, bf16[512,512]{1,0:T(8,128)(2,1)S(1)}, u32[]{:S(2)}, u32[]{:S(2)}) %collective-permute-start) | collective-permute-done | bytes 524320 | tf_op jit(solution)/shard_map/ppermute | solution.py:133
  130.7 1.2 collective-permute-done.1
  132.3 1.9 fusion.61
  134.8 1.3 pad_maximum_fusion
  136.1 83.8 %all-reduce.2.cloned.1.call-done = f32[768,512]{1,0:T(8,128)} async-done(((f32[768,512]{1,0:T(8,128)}), f32[768,512]{1,0:T(8,128)}) %all-reduce.2.cloned.1.call-update) | async-done | bytes 1572880 | tf_op jit(solution)/shard_map/psum | solution.py:149
  219.9 1.0 slice.123
  220.9 11.7 %custom-call.6 = f32[128,128]{1,0:T(8,128)S(1)} custom-call(f32[128,128]{1,0:T(8,128)S(1)} %slice.123), custom_call_target="Cholesky" | custom-call | tf_op jit(solution)/shard_map/cholesky/custom-call.1 | solution.py:64
  234.0 0.9 fusion.56
  238.9 11.9 %custom-call.7 = f32[128,128]{1,0:T(8,128)S(1)} custom-call(f32[128,128]{1,0:T(8,128)S(1)} %slice.129), custom_call_target="Cholesky" | custom-call | tf_op jit(solution)/shard_map/cholesky/custom-call.1 | solution.py:64
  252.2 0.9 fusion.57
  257.1 11.7 %custom-call.8 = f32[128,128]{1,0:T(8,128)S(1)} custom-call(f32[128,128]{1,0:T(8,128)S(1)} %slice.137), custom_call_target="Cholesky" | custom-call | tf_op jit(solution)/shard_map/cholesky/custom-call.1 | solution.py:64
  270.3 0.9 fusion.58
  275.0 11.9 %custom-call.9 = f32[128,128]{1,0:T(8,128)S(1)} custom-call(f32[128,128]{1,0:T(8,128)S(1)} %convolution_subtract_fusion.8), custom_call_target="Cholesky" | custom-call | tf_op jit(solution)/shard_map/cholesky/custom-call.1 | solution.py:64
  288.4 0.9 fusion.59
  289.3 0.9 convolution_add_fusion.5
  299.3 1.0 copy.11
  300.4 1.0 copy.10
  (102 shorter events, 29.4 us)
Async XLA Ops:
  7.2 52.9 %all-gather.6.cloned.1.call-start = ((), (), s32[]{:S(2)}) async-start(), calls=%async_computation.1 | async-start | bytes 4456448 | tf_op jit(solution)/shard_map/all_gather | solution.py:107
  7.9 97.3 %all-gather.8.cloned.1.call-start = ((), (), s32[]{:S(2)}) async-start(), calls=%async_computation.2 | async-start | bytes 4456448 | tf_op jit(solution)/shard_map/all_gather | solution.py:107
  8.6 211.3 %all-reduce.2.cloned.1.call-start = ((), (), s32[]{:S(2)}) async-start(), calls=%async_computation | async-start | bytes 3145728 | tf_op jit(solution)/shard_map/psum | solution.py:149
  105.2 9.2 %copy-start = (bf16[1,512,512]{2,1,0:T(8,128)(2,1)S(1)}, bf16[1,512,512]{2,1,0:T(8,128)(2,1)}, u32[]{:S(2)}) copy-start(bf16[1,512,512]{2,1,0:T(8,128)(2,1)} %param.8) | copy-start | bytes 1572868
  114.7 16.0 %collective-permute-start = (bf16[512,512]{1,0:T(8,128)(2,1)S(1)}, bf16[512,512]{1,0:T(8,128)(2,1)S(1)}, u32[]{:S(2)}, u32[]{:S(2)}) collective-permute-start(bf16[512,512]{1,0:T(8,128)(2,1)S(1)} %fusion.60), channel_id=1, source_target_pairs={{0,1},{1,2},{2,3},{4,5},{5,6},{6,7},{8,9},{9,10},{10,11},{12,13},{... | collective-permute-start | bytes 1572872 | tf_op jit(solution)/shard_map/ppermute | solution.py:133
  116.0 15.8 %collective-permute-start.1 = (bf16[512,512]{1,0:T(8,128)(2,1)S(1)}, bf16[512,512]{1,0:T(8,128)(2,1)S(1)}, u32[]{:S(2)}, u32[]{:S(2)}) collective-permute-start(bf16[512,512]{1,0:T(8,128)(2,1)S(1)} %fusion.60), channel_id=1, source_target_pairs={{1,0},{2,1},{3,2},{5,4},{6,5},{7,6},{9,8},{10,9},{11,10},{13,12},{... | collective-permute-start | bytes 1572872 | tf_op jit(solution)/shard_map/ppermute | solution.py:134
  132.3 1.9 copy-start.1
  219.9 18.1 %copy-start.2 = (f32[768,512]{1,0:T(8,128)S(1)}, f32[768,512]{1,0:T(8,128)}, u32[]{:S(2)}) copy-start(f32[768,512]{1,0:T(8,128)} %all-reduce.2.cloned.1.call-done) | copy-start | bytes 4718596
Sparse Core Ops, SparseCore 0:
  10.1 49.9 all-gather.5
  62.2 42.9 all-gather.7
  136.3 83.6 all-reduce.1

commit v7 on v5

--- a/solution.py
+++ b/solution.py
@@ -33,7 +33,7 @@
 
 
 def lower_inverse(factor):
-    hi = lax.Precision.HIGHEST
+    hi = lax.Precision.HIGH
     size = factor.shape[0]
     eye = jnp.eye(size, dtype=factor.dtype)
     scale = jnp.sum(factor * eye, axis=1)
@@ -51,7 +51,7 @@
 def blocked_factor(gram, block):
     size = gram.shape[0]
     count = size // block
-    hi = lax.Precision.HIGHEST
+    hi = lax.Precision.HIGH
     eye = jnp.eye(block, dtype=gram.dtype)
     columns = []
     inverses = []
@@ -73,7 +73,7 @@
 
 
 def right_solve(values, columns, inverses, block):
-    hi = lax.Precision.HIGHEST
+    hi = lax.Precision.HIGH
     parts = []
     for j, inverse in enumerate(inverses):
         top = j * block

time: 281 us -> 273 us (0.972); the launches traced: 277 us -> 273 us
  matrix products: 31.8 us -> 27.6 us
where the time goes in v7:
time: 273 us
  waiting for transfers between devices  137 us (50%)
  other arithmetic  60.3 us (22%)
  matrix products  27.6 us (10%)
  blocking collectives  23.5 us (9%)
  between operations  14.8 us (5%)
  starting transfers between devices  4.54 us (2%)
  local copies, waits for them, and re-layouts  4.48 us (2%)
    psum x1, waiting for transfers between devices, body(): summed = lax.psum(jnp.concatenate([local_gram, local_proj], axis=0), 'rx')  81.6 us
    another operation x12, other arithmetic, blocked_factor(): diag = lax.linalg.cholesky(panel[:block], symmetrize_input=False)  49.7 us
    all_gather x1, waiting for transfers between devices, body(): lax.all_gather(jnp.concatenate([block_data, block_test], axis=1), 'tm', a...  41.5 us
    all_gather x1, blocking collectives, body(): decays = lax.all_gather(own_decay, 'tm', axis=0)  23.5 us
    ppermute x1, waiting for transfers between devices, body(): above = lax.ppermute(sent, 'bin', downward).astype(jnp.float32)  10.1 us
    dot_general x24, matrix products, lower_inverse(): power = jnp.dot(power, power, precision=hi)  7.13 us
    dot_general x24, matrix products, lower_inverse(): total = total + jnp.dot(total, power, precision=hi)  7.08 us
  transfers between devices with their start and end apart: 4, of which 4 were waited for; matrix products, arithmetic and copies ran while one was open for 0% of the time, Pallas kernels for 0%

profile of v7, /device:TPU:6, one launch (start us, length us, event | category | flops | bytes accessed | tf_op | source)
XLA Modules:
  0.0 272.6 jit_solution(604300182297209460)
XLA Ops:
  7.2 1.9 pad_maximum_fusion.2
  9.2 23.5 %all-gather = f32[16,1,512]{2,1,0:T(1,128)S(1)} all-gather(f32[1,1,512]{2,1,0:T(1,128)} %param.7), channel_id=2, replica_groups=mesh['rx'=8,'tm'=16,'bin'=4] {'tm'}, dimensions={0}, use_global_device_ids=true | all-gather | bytes 34816 | tf_op jit(solution)/shard_map/all_gather | solution.py:112
  33.0 41.5 %all-gather.3.cloned.1.call-done = bf16[4096,1024]{1,0:T(8,128)(2,1)} async-done(((bf16[256,1024]{1,0:T(8,128)(2,1)}), bf16[4096,1024]{1,0:T(8,128)(2,1)}) %all-gather.3.cloned.1.call-update) | async-done | bytes 8388624 | tf_op jit(solution)/shard_map/all_gather | solution.py:107
  74.6 3.2 %reduce-precision_convert_fusion = (bf16[4096,512]{1,0:T(8,128)(2,1)S(1)}, bf16[4096,512]{1,0:T(8,128)(2,1)S(1)}) fusion(f32[16,512]{1,0:T(8,128)S(1)} %broadcast_select_fusion, bf16[4096,1024]{1,0:T(8,128)(2,1)} %all-gather.3.cloned.1.call-done), kind=kLoop, calls=%fused_computation.1 | loop fusion | flops 12582912 | bytes 12615680 | tf_op jit(solution)/shard_map/convert_element_type | solution.py:124
  77.8 1.4 copy-done.2
  79.2 4.5 %fusion.1 = f32[512,1024]{1,0:T(8,128)S(1)} fusion(bf16[4096,512]{1,0:T(8,128)(2,1)S(1)} %get-tuple-element.10, bf16[4096,512]{1,0:T(8,128)(2,1)S(1)} %get-tuple-element.9, bf16[4096,1024]{1,0:T(8,128)(2,1)S(1)} %copy-done.2), kind=kOutput, calls=%fused_computation.3 | convolution fusion | flops 4311744512 | bytes 14680064 | tf_op jit(solution)/shard_map/dot_general | solution.py:126
  84.1 3.0 %collective-permute-start.1 = (bf16[512,512]{1,0:T(8,128)(2,1)S(1)}, bf16[512,512]{1,0:T(8,128)(2,1)S(1)}, u32[]{:S(2)}, u32[]{:S(2)}) collective-permute-start(bf16[512,512]{1,0:T(8,128)(2,1)S(1)} %fusion.55), channel_id=1, source_target_pairs={{1,0},{2,1},{3,2},{5,4},{6,5},{7,6},{9,8},{10,9},{11,10},{13,12},{... | collective-permute-start | bytes 1572872 | tf_op jit(solution)/shard_map/ppermute | solution.py:138
  87.1 1.5 collective-permute-start
  88.5 10.1 %collective-permute-done.1 = bf16[512,512]{1,0:T(8,128)(2,1)S(1)} collective-permute-done((bf16[512,512]{1,0:T(8,128)(2,1)S(1)}, bf16[512,512]{1,0:T(8,128)(2,1)S(1)}, u32[]{:S(2)}, u32[]{:S(2)}) %collective-permute-start.1) | collective-permute-done | bytes 524320 | tf_op jit(solution)/shard_map/ppermute | solution.py:138
  98.6 4.1 %collective-permute-done = bf16[512,512]{1,0:T(8,128)(2,1)S(1)} collective-permute-done((bf16[512,512]{1,0:T(8,128)(2,1)S(1)}, bf16[512,512]{1,0:T(8,128)(2,1)S(1)}, u32[]{:S(2)}, u32[]{:S(2)}) %collective-permute-start) | collective-permute-done | bytes 524320 | tf_op jit(solution)/shard_map/ppermute | solution.py:137
  103.8 1.9 fusion.56
  105.7 1.3 pad_maximum_fusion
  107.0 81.6 %all-reduce.2.cloned.1.call-done = f32[768,512]{1,0:T(8,128)} async-done(((f32[768,512]{1,0:T(8,128)}), f32[768,512]{1,0:T(8,128)}) %all-reduce.2.cloned.1.call-update) | async-done | bytes 1572880 | tf_op jit(solution)/shard_map/psum | solution.py:153
  188.6 1.0 slice.133
  189.5 11.7 %custom-call.6 = f32[128,128]{1,0:T(8,128)S(1)} custom-call(f32[128,128]{1,0:T(8,128)S(1)} %slice.133), custom_call_target="Cholesky" | custom-call | tf_op jit(solution)/shard_map/cholesky/custom-call.1 | solution.py:64
  202.7 0.9 fusion.51
  207.0 11.8 %custom-call.7 = f32[128,128]{1,0:T(8,128)S(1)} custom-call(f32[128,128]{1,0:T(8,128)S(1)} %slice.139), custom_call_target="Cholesky" | custom-call | tf_op jit(solution)/shard_map/cholesky/custom-call.1 | solution.py:64
  220.3 0.9 fusion.52
  224.6 11.7 %custom-call.8 = f32[128,128]{1,0:T(8,128)S(1)} custom-call(f32[128,128]{1,0:T(8,128)S(1)} %slice.147), custom_call_target="Cholesky" | custom-call | tf_op jit(solution)/shard_map/cholesky/custom-call.1 | solution.py:64
  237.8 0.9 fusion.53
  242.0 11.7 %custom-call.9 = f32[128,128]{1,0:T(8,128)S(1)} custom-call(f32[128,128]{1,0:T(8,128)S(1)} %convolution_subtract_fusion.8), custom_call_target="Cholesky" | custom-call | tf_op jit(solution)/shard_map/cholesky/custom-call.1 | solution.py:64
  255.2 0.9 fusion.54
  263.7 1.0 copy.10
  264.7 1.0 copy.11
  (107 shorter events, 24.8 us)
Async XLA Ops:
  7.2 67.4 %all-gather.3.cloned.1.call-start = ((), (), s32[]{:S(2)}) async-start(), calls=%async_computation | async-start | bytes 8912896 | tf_op jit(solution)/shard_map/all_gather | solution.py:107
  9.1 179.5 %all-reduce.2.cloned.1.call-start = ((), (), s32[]{:S(2)}) async-start(), calls=%async_computation.1 | async-start | bytes 3145728 | tf_op jit(solution)/shard_map/psum | solution.py:153
  74.6 4.7 %copy-start.2 = (bf16[4096,1024]{1,0:T(8,128)(2,1)S(1)}, bf16[4096,1024]{1,0:T(8,128)(2,1)}, u32[]{:S(2)}) copy-start(bf16[4096,1024]{1,0:T(8,128)(2,1)} %all-gather.3.cloned.1.call-done) | copy-start | bytes 25165828
  79.2 4.5 %copy-start.3 = (bf16[1,512,512]{2,1,0:T(8,128)(2,1)S(1)}, bf16[1,512,512]{2,1,0:T(8,128)(2,1)}, u32[]{:S(2)}) copy-start(bf16[1,512,512]{2,1,0:T(8,128)(2,1)} %param.8) | copy-start | bytes 1572868
  84.1 19.1 %copy-start.4 = (bf16[1,256,512]{2,1,0:T(8,128)(2,1)S(1)}, bf16[1,256,512]{2,1,0:T(8,128)(2,1)}, u32[]{:S(2)}) copy-start(bf16[1,256,512]{2,1,0:T(8,128)(2,1)} %param.5) | copy-start | bytes 786436
  84.1 14.5 %collective-permute-start.1 = (bf16[512,512]{1,0:T(8,128)(2,1)S(1)}, bf16[512,512]{1,0:T(8,128)(2,1)S(1)}, u32[]{:S(2)}, u32[]{:S(2)}) collective-permute-start(bf16[512,512]{1,0:T(8,128)(2,1)S(1)} %fusion.55), channel_id=1, source_target_pairs={{1,0},{2,1},{3,2},{5,4},{6,5},{7,6},{9,8},{10,9},{11,10},{13,12},{... | collective-permute-start | bytes 1572872 | tf_op jit(solution)/shard_map/ppermute | solution.py:138
  87.1 15.7 %collective-permute-start = (bf16[512,512]{1,0:T(8,128)(2,1)S(1)}, bf16[512,512]{1,0:T(8,128)(2,1)S(1)}, u32[]{:S(2)}, u32[]{:S(2)}) collective-permute-start(bf16[512,512]{1,0:T(8,128)(2,1)S(1)} %fusion.55), channel_id=1, source_target_pairs={{0,1},{1,2},{2,3},{4,5},{5,6},{6,7},{8,9},{9,10},{10,11},{12,13},{... | collective-permute-start | bytes 1572872 | tf_op jit(solution)/shard_map/ppermute | solution.py:137
  188.6 17.8 %copy-start.5 = (f32[768,512]{1,0:T(8,128)S(1)}, f32[768,512]{1,0:T(8,128)}, u32[]{:S(2)}) copy-start(f32[768,512]{1,0:T(8,128)} %all-reduce.2.cloned.1.call-done) | copy-start | bytes 4718596
  206.6 17.6 %copy-start = (f32[384,128]{0,1:T(8,128)}, f32[384,128]{0,1:T(8,128)S(1)}, u32[]{:S(2)}) copy-start(f32[384,128]{0,1:T(8,128)S(1)} %fusion.25) | copy-start | bytes 589828
  224.6 17.0 %slice-start = ((f32[384,128]{0,1:T(8,128)}), f32[128,128]{0,1:T(8,128)S(1)}, s32[]{:S(2)}) async-start(f32[384,128]{0,1:T(8,128)} %copy-done), calls=%async_computation.2 | async-start | bytes 131072 | tf_op jit(solution)/shard_map/slice | solution.py:83
  242.0 15.5 %copy-start.1 = (f32[384,128]{0,1:T(8,128)S(1)}, f32[384,128]{0,1:T(8,128)}, u32[]{:S(2)}) copy-start(f32[384,128]{0,1:T(8,128)} %copy-done) | copy-start | bytes 589828
Sparse Core Ops, SparseCore 0:
  10.7 63.8 all-gather.2
  107.1 81.4 all-reduce.1
